TPU v7x, 128 devices: a whole 4x4x4 slice. The times are simulated.
128 devices in a mesh: ctx: 64 (over x, y_lo, z, core), tp: 2 (over y_hi).
Axes of the slice: x: 4, y: 4 (y_hi: 2, y_lo: 2; y = y_hi * 2 + y_lo), z: 4, core: 2. Of those that a mesh axis runs over, the one named last changes fastest.
Arguments:
- rotated_queries: bfloat16 [8192, 2048], P('ctx', 'tp'), may hold values from -150 to 150
- rotated_keys: bfloat16 [8192, 1024], P('ctx', 'tp'), may hold values from -5 to 5
- value_matrix: bfloat16 [8192, 1024], P('ctx', 'tp'), may hold values from -6 to 6
- out_grad: bfloat16 [8192, 5376], P('ctx', 'tp'), may hold values from -16 to 16
- out_weight: bfloat16 [2048, 5376], P('tp', 'ctx'), may hold values from -0.125 to 0.125
Outputs:
- query_grad: bfloat16 [8192, 2048], P('ctx', 'tp')
- key_gradient: bfloat16 [8192, 1024], P('ctx', 'tp')
- value_gradient: bfloat16 [8192, 1024], P('ctx', 'tp')
- weight_grad: float32 [2048, 5376], P('tp', 'ctx')
All inputs are finite; a program needn't handle non-finite values.
Results may differ from a plain program's by a relative error of at most 0.013.
The roundings to bfloat16 on the way count: a program that leaves them out, or rounds other values in their place, can miss the bound.
Values may be sent and summed in bfloat16 or wider, within the bound.
No kernel may reach another device: no remote copies, remote signals or barrier semaphores. Data moves between devices by JAX's collectives and lax.ppermute only.
A program may use at most 128 MiB of HBM per device.

v0:
```python
import jax
import jax.numpy as jnp
from jax import lax
from jax.sharding import PartitionSpec as P

HEAD_SIZE = 128
WINDOW_SPAN = 1024
QUERY_HEAD_COUNT = 16
KEY_VALUE_HEADS = 8


score_scale = 168.0 ** (-0.5)


def from_behind(block, axis, distance):
    devices = range(lax.axis_size(axis))
    route = [(i - distance, i) for i in devices if i - distance in devices]
    return lax.ppermute(block, axis, route)


def band_mask(query_pos, key_pos):
    earlier = key_pos[None, :] <= query_pos[:, None]
    within = query_pos[:, None] - key_pos[None, :] < WINDOW_SPAN
    return earlier & within & (key_pos[None, :] >= 0)


def scores_for(query_head, key_head, allowed):
    scaled = (
        jnp.einsum("tgd,kd->gtk", query_head, key_head, preferred_element_type=jnp.float32)
        * score_scale
    )
    return jnp.where(allowed[None], scaled, -jnp.inf)


def forward_head(query_head, key_head, value_head, allowed):
    scores = scores_for(query_head, key_head, allowed)
    row_max = jnp.max(scores, axis=-1, keepdims=True)
    log_total = row_max + jnp.log(jnp.sum(jnp.exp(scores - row_max), axis=-1, keepdims=True))
    probs = jnp.exp(scores - log_total).astype(jnp.bfloat16)
    output = jnp.einsum("gtk,kd->tgd", probs, value_head, preferred_element_type=jnp.float32)
    return (output.astype(jnp.bfloat16), log_total[..., 0])


def grad_band(query_head, grad_head, log_total, delta_head, key_head, value_head, allowed):
    scores = scores_for(query_head, key_head, allowed)
    probs = jnp.exp(scores - log_total[..., None])
    probs_low = probs.astype(jnp.bfloat16)
    prob_grad = jnp.einsum("tgd,kd->gtk", grad_head, value_head, preferred_element_type=jnp.float32)
    score_grad = (probs * (prob_grad - delta_head.T[..., None])).astype(jnp.bfloat16)
    query_part = (
        jnp.einsum("gtk,kd->tgd", score_grad, key_head, preferred_element_type=jnp.float32)
        * score_scale
    )
    key_part = (
        jnp.einsum("gtk,tgd->kd", score_grad, query_head, preferred_element_type=jnp.float32)
        * score_scale
    )
    value_part = jnp.einsum("gtk,tgd->kd", probs_low, grad_head, preferred_element_type=jnp.float32)
    return (query_part, key_part, value_part)


def per_device(rotated_queries, rotated_keys, value_matrix, out_grad, out_weight):
    tokens_dev = rotated_queries.shape[0]
    n_ctx = lax.axis_size("ctx")
    kv_local = rotated_keys.shape[1] // HEAD_SIZE
    group_width = QUERY_HEAD_COUNT // KEY_VALUE_HEADS
    reach_count = WINDOW_SPAN // tokens_dev
    start_pos = lax.axis_index("ctx") * tokens_dev
    query_pos = start_pos + jnp.arange(tokens_dev, dtype=jnp.int32)
    earlier = []
    for offset in range(reach_count, 0, -1):
        earlier.append(from_behind((rotated_keys, value_matrix), "ctx", offset))
    key_ext = jnp.concatenate([pair[0] for pair in earlier] + [rotated_keys], 0)
    value_ext = jnp.concatenate([pair[1] for pair in earlier] + [value_matrix], 0)
    key_pos = (
        start_pos
        - reach_count * tokens_dev
        + jnp.arange((reach_count + 1) * tokens_dev, dtype=jnp.int32)
    )
    full_mask = band_mask(query_pos, key_pos)
    query_heads = rotated_queries.reshape(tokens_dev, kv_local, group_width, HEAD_SIZE).transpose(
        1, 0, 2, 3
    )
    key_heads = key_ext.reshape(-1, kv_local, HEAD_SIZE).transpose(1, 0, 2)
    value_heads = value_ext.reshape(-1, kv_local, HEAD_SIZE).transpose(1, 0, 2)
    attn_heads, log_totals = lax.map(
        lambda items: forward_head(items[0], items[1], items[2], full_mask),
        (query_heads, key_heads, value_heads),
    )
    attn_rows = attn_heads.transpose(1, 0, 2, 3)
    attention_probs = attn_rows.reshape(tokens_dev, -1)
    cotangent = lax.all_gather(out_grad, "tp", axis=1, tiled=True)
    grad_sum = lax.dot_general(
        cotangent,
        lax.all_gather(out_weight, "ctx", axis=1, tiled=True),
        (((1,), (1,)), ((), ())),
        preferred_element_type=jnp.float32,
    )
    attention_gradient = grad_sum.astype(jnp.bfloat16)
    weight_term = jnp.dot(attention_probs.T, cotangent, preferred_element_type=jnp.float32) * (
        tokens_dev * n_ctx
    ) ** (-0.5)
    weight_grad = lax.psum_scatter(weight_term, "ctx", scatter_dimension=1, tiled=True)
    grad_rows = attention_gradient.reshape(tokens_dev, kv_local, group_width, HEAD_SIZE)
    row_deltas = jnp.sum(grad_rows.astype(jnp.float32) * attn_rows.astype(jnp.float32), axis=-1)
    head_gradients = grad_rows.transpose(1, 0, 2, 3)
    delta_heads = row_deltas.transpose(1, 0, 2)
    query_parts, key_parts, value_parts = lax.map(
        lambda items: grad_band(
            items[0], items[1], items[2], items[3], items[4], items[5], full_mask
        ),
        (query_heads, head_gradients, log_totals, delta_heads, key_heads, value_heads),
    )
    key_ext_grad = key_parts.transpose(1, 0, 2).reshape(-1, kv_local * HEAD_SIZE)
    value_ext_grad = value_parts.transpose(1, 0, 2).reshape(-1, kv_local * HEAD_SIZE)
    key_total = key_ext_grad[reach_count * tokens_dev :]
    value_total = value_ext_grad[reach_count * tokens_dev :]
    for offset in range(1, reach_count + 1):
        first_row = (reach_count - offset) * tokens_dev
        back_key, back_value = from_behind(
            (
                key_ext_grad[first_row : first_row + tokens_dev],
                value_ext_grad[first_row : first_row + tokens_dev],
            ),
            "ctx",
            -offset,
        )
        key_total = key_total + back_key
        value_total = value_total + back_value
    query_grad = query_parts.transpose(1, 0, 2, 3).reshape(tokens_dev, -1).astype(jnp.bfloat16)
    return (
        query_grad,
        key_total.astype(jnp.bfloat16),
        value_total.astype(jnp.bfloat16),
        weight_grad,
    )


def solution(mesh):
    placed = (P("ctx", "tp"), P("ctx", "tp"), P("ctx", "tp"), P("ctx", "tp"), P("tp", "ctx"))
    return jax.shard_map(
        per_device,
        mesh=mesh,
        in_specs=placed,
        out_specs=(P("ctx", "tp"), P("ctx", "tp"), P("ctx", "tp"), P("tp", "ctx")),
        check_vma=False,
    )
```

profile of v0, /device:TPU:8, one launch (start us, length us, event | category | flops | bytes accessed | tf_op | source)
XLA Modules:
  0.0 488.3 jit_solution(3301119252186643372)
XLA Ops:
  10.9 3.8 collective-permute-start.14
  14.7 4.9 collective-permute-start.13
  20.7 4.0 collective-permute-start.1
  24.7 3.5 collective-permute-start
  28.7 7.0 %collective-permute-done = bf16[128,512]{0,1:T(8,128)(2,1)S(1)} collective-permute-done((bf16[128,512]{0,1:T(8,128)(2,1)S(1)}, bf16[128,512]{0,1:T(8,128)(2,1)S(1)}, u32[]{:S(2)}, u32[]{:S(2)}) %collective-permute-start) | collective-permute-done | bytes 131104 | tf_op jit(solution)/shard_map/ppermute | solution.py:18
  35.7 4.1 collective-permute-start.2
  42.3 5.4 %collective-permute-done.2 = bf16[128,512]{0,1:T(8,128)(2,1)S(1)} collective-permute-done((bf16[128,512]{0,1:T(8,128)(2,1)S(1)}, bf16[128,512]{0,1:T(8,128)(2,1)S(1)}, u32[]{:S(2)}, u32[]{:S(2)}) %collective-permute-start.2) | collective-permute-done | bytes 131104 | tf_op jit(solution)/shard_map/ppermute | solution.py:18
  47.7 4.7 collective-permute-start.4
  56.9 4.3 collective-permute-start.6
  70.7 5.0 %collective-permute-start.8 = (bf16[128,512]{0,1:T(8,128)(2,1)S(1)}, bf16[128,512]{0,1:T(8,128)(2,1)S(1)}, u32[]{:S(2)}, u32[]{:S(2)}) collective-permute-start(bf16[128,512]{0,1:T(8,128)(2,1)S(1)} %copy.95), channel_id=1, source_target_pairs={{0,16},{2,18},{4,20},{6,22},{8,24},{10,26},{12,28},{14,30},{16,32}... | collective-permute-start | bytes 393224 | tf_op jit(solution)/shard_map/ppermute | solution.py:18
  75.8 5.0 %collective-permute-done.8 = bf16[128,512]{0,1:T(8,128)(2,1)S(1)} collective-permute-done((bf16[128,512]{0,1:T(8,128)(2,1)S(1)}, bf16[128,512]{0,1:T(8,128)(2,1)S(1)}, u32[]{:S(2)}, u32[]{:S(2)}) %collective-permute-start.8) | collective-permute-done | bytes 131104 | tf_op jit(solution)/shard_map/ppermute | solution.py:18
  88.7 5.5 %collective-permute-start.12 = (bf16[128,512]{0,1:T(8,128)(2,1)S(1)}, bf16[128,512]{0,1:T(8,128)(2,1)S(1)}, u32[]{:S(2)}, u32[]{:S(2)}) collective-permute-start(bf16[128,512]{0,1:T(8,128)(2,1)S(1)} %copy.95), channel_id=1, source_target_pairs={{0,8},{2,10},{4,12},{6,14},{8,16},{10,18},{12,20},{14,22},{16,24},... | collective-permute-start | bytes 393224 | tf_op jit(solution)/shard_map/ppermute | solution.py:18
  94.3 4.6 collective-permute-done.12
  102.6 7.3 %while.28 = (s32[]{:T(128)}, bf16[4,128,2,128]{1,3,2,0:T(8,128)(2,1)S(1)}, f32[4,2,128]{2,1,0:T(2,128)S(1)}, bf16[4,1152,128]{1,2,0:T(8,128)(2,1)S(1)}, bf16[4,1...) while((s32[]{:T(128)}, ...), condition=%wide.region_3.4_spmd.clone, body=%wide.region_0.3_spmd.clone.sunk | while | flops 153829120 | bytes 4571377 | solution.py:86
  110.0 10.9 %convolution_multiply_fusion.3 = f32[1024,5376]{0,1:T(8,128)} fusion(bf16[128,1024]{0,1:T(8,128)(2,1)S(1)} %bitcast.298, bf16[128,5376]{1,0:T(8,128)(2,1)} %all-gather.4.cloned.1.call-done), kind=kOutput, calls=%fused_computation.69 | convolution fusion | flops 1414791168 | bytes 23658496 | tf_op jit(solution)/shard_map/dot_general | solution.py:100
  120.9 172.5 %fusion.4 = f32[1024,88]{0,1:T(8,128)S(1)} fusion(f32[1024,5376]{0,1:T(8,128)} %convolution_multiply_fusion.3), kind=kCustom, calls=%all-reduce-scatter | all-reduce-scatter fusion | flops 5767169 | bytes 22381056
  294.2 6.2 %collective-permute-start.33 = (f32[1024,88]{0,1:T(8,128)S(1)}, f32[1024,88]{0,1:T(8,128)}, u32[]{:S(2)}, u32[]{:S(2)}) collective-permute-start(f32[1024,88]{0,1:T(8,128)S(1)} %fusion.4), channel_id=1, source_target_pairs={{0,4},{2,6},{4,8},{6,10},{8,12},{10,14},{12,16},{14,18},{16,20},{1... | collective-permute-start | bytes 1081352
  300.4 5.4 %collective-permute-start.32 = (f32[1024,88]{0,1:T(8,128)S(1)}, f32[1024,88]{0,1:T(8,128)}, u32[]{:S(2)}, u32[]{:S(2)}) collective-permute-start(f32[1024,88]{0,1:T(8,128)S(1)} %fusion.4), channel_id=1, source_target_pairs={{0,2},{2,4},{4,6},{6,8},{8,10},{10,12},{12,14},{14,16},{16,18},{18... | collective-permute-start | bytes 1081352
  305.8 10.4 %collective-permute-start.34 = (f32[1024,76]{0,1:T(8,128)}, f32[1024,76]{0,1:T(8,128)}, u32[]{:S(2)}, u32[]{:S(2)}) collective-permute-start(f32[1024,76]{0,1:T(8,128)} %slice.162), channel_id=1, source_target_pairs={{0,6},{2,8},{4,10},{6,12},{8,14},{10,16},{12,18},{14,20},{16,22},{... | collective-permute-start | bytes 933896
  316.3 14.0 %reshape.94 = bf16[5376,1024]{1,0:T(8,128)(2,1)} reshape(bf16[64,84,1024]{2,1,0:T(8,128)(2,1)} %all-gather.6.cloned.1.call-done) | data formatting | bytes 22020096
  330.3 6.4 %convolution_convert_fusion.1 = bf16[128,1024]{1,0:T(8,128)(2,1)} fusion(bf16[128,5376]{1,0:T(8,128)(2,1)S(1)} %copy-done, bf16[5376,1024]{1,0:T(8,128)(2,1)} %reshape.94), kind=kOutput, calls=%fused_computation.70 | convolution fusion | flops 1409417216 | bytes 12648448 | tf_op jit(solution)/shard_map/dot_general | solution.py:93
  338.2 23.4 %while.29 = (s32[]{:T(128)}, bf16[4,128,2,128]{1,3,2,0:T(8,128)(2,1)}, f32[4,1152,128]{2,1,0:T(8,128)}, f32[4,1152,128]{2,1,0:T(8,128)}, bf16[4,1152,128]{2,1,0:...) while((s32[]{:T(128)}, ...), condition=%wide.region_6.7_spmd.clone, body=%wide.region_5.6_spmd.clone.sunk | while | flops 380469248 | bytes 8078613 | solution.py:108
  371.8 8.6 %collective-permute-start.27 = (f32[128,512]{1,0:T(8,128)S(1)}, f32[128,512]{1,0:T(8,128)}, u32[]{:S(2)}, u32[]{:S(2)}) collective-permute-start(f32[128,512]{1,0:T(8,128)S(1)} %bitcast.304), channel_id=1, source_target_pairs={{8,0},{10,2},{12,4},{14,6},{16,8},{18,10},{20,12},{22,14},{24,16},... | collective-permute-start | bytes 786440 | tf_op jit(solution)/shard_map/ppermute | solution.py:18
  389.4 3.3 collective-permute-done.26
  392.7 5.0 %collective-permute-start.31 = (f32[128,512]{1,0:T(8,128)}, f32[128,512]{1,0:T(8,128)}, u32[]{:S(2)}, u32[]{:S(2)}) collective-permute-start(f32[128,512]{1,0:T(8,128)} %bitcast.232), channel_id=1, source_target_pairs={{16,0},{18,2},{20,4},{22,6},{24,8},{26,10},{28,12},{30,14},{32,16}... | collective-permute-start | bytes 786440 | tf_op jit(solution)/shard_map/ppermute | solution.py:18
  397.7 6.2 %collective-permute-done.27 = f32[128,512]{1,0:T(8,128)} collective-permute-done((f32[128,512]{1,0:T(8,128)S(1)}, f32[128,512]{1,0:T(8,128)}, u32[]{:S(2)}, u32[]{:S(2)}) %collective-permute-start.27) | collective-permute-done | bytes 262176 | tf_op jit(solution)/shard_map/ppermute | solution.py:18
  411.4 3.5 concatenate.8
  419.7 3.2 collective-permute-done.31
  436.0 6.3 %collective-permute-done.20 = f32[128,512]{1,0:T(8,128)S(1)} collective-permute-done((f32[128,512]{1,0:T(8,128)S(1)}, f32[128,512]{1,0:T(8,128)S(1)}, u32[]{:S(2)}, u32[]{:S(2)}) %collective-permute-start.20) | collective-permute-done | bytes 262176 | tf_op jit(solution)/shard_map/ppermute | solution.py:18
  442.3 5.6 %collective-permute-done.21 = f32[128,512]{1,0:T(8,128)S(1)} collective-permute-done((f32[128,512]{1,0:T(8,128)S(1)}, f32[128,512]{1,0:T(8,128)S(1)}, u32[]{:S(2)}, u32[]{:S(2)}) %collective-permute-start.21) | collective-permute-done | bytes 262176 | tf_op jit(solution)/shard_map/ppermute | solution.py:18
  447.9 5.6 %collective-permute-done.22 = f32[128,512]{1,0:T(8,128)S(1)} collective-permute-done((f32[128,512]{1,0:T(8,128)S(1)}, f32[128,512]{1,0:T(8,128)S(1)}, u32[]{:S(2)}, u32[]{:S(2)}) %collective-permute-start.22) | collective-permute-done | bytes 262176 | tf_op jit(solution)/shard_map/ppermute | solution.py:18
  453.6 26.0 %collective-permute-done.23 = f32[128,512]{1,0:T(8,128)S(1)} collective-permute-done((f32[128,512]{1,0:T(8,128)S(1)}, f32[128,512]{1,0:T(8,128)S(1)}, u32[]{:S(2)}, u32[]{:S(2)}) %collective-permute-start.23) | collective-permute-done | bytes 262176 | tf_op jit(solution)/shard_map/ppermute | solution.py:18
  (188 shorter events, 111.2 us)
Async XLA Ops:
  7.2 102.8 %all-gather.4.cloned.1.call-start = ((), (), s32[]{:S(2)}) async-start(), calls=%async_computation | async-start | bytes 2064384 | tf_op jit(solution)/shard_map/all_gather | solution.py:92
  7.9 308.4 %all-gather.6.cloned.1.call-start = ((), (), s32[]{:S(2)}) async-start(), calls=%async_computation.1 | async-start | bytes 11714560 | tf_op jit(solution)/shard_map/all_gather | solution.py:95
  9.0 92.6 %collective-permute-start.15 = (bf16[128,512]{0,1:T(8,128)(2,1)S(1)}, bf16[128,512]{0,1:T(8,128)(2,1)}, u32[]{:S(2)}, u32[]{:S(2)}) collective-permute-start(bf16[128,512]{0,1:T(8,128)(2,1)S(1)} %copy.95), channel_id=1, source_target_pairs={{0,2},{2,4},{4,6},{6,8},{8,10},{10,12},{12,14},{14,16},{16,18},{18... | collective-permute-start | bytes 393224 | tf_op jit(solution)/shard_map/ppermute | solution.py:18
  10.9 89.7 %collective-permute-start.14 = (bf16[128,512]{0,1:T(8,128)(2,1)S(1)}, bf16[128,512]{0,1:T(8,128)(2,1)}, u32[]{:S(2)}, u32[]{:S(2)}) collective-permute-start(bf16[128,512]{0,1:T(8,128)(2,1)S(1)} %copy.95), channel_id=1, source_target_pairs={{0,4},{2,6},{4,8},{6,10},{8,12},{10,14},{12,16},{14,18},{16,20},{1... | collective-permute-start | bytes 393224 | tf_op jit(solution)/shard_map/ppermute | solution.py:18
  14.7 84.1 %collective-permute-start.13 = (bf16[128,512]{0,1:T(8,128)(2,1)S(1)}, bf16[128,512]{0,1:T(8,128)(2,1)S(1)}, u32[]{:S(2)}, u32[]{:S(2)}) collective-permute-start(bf16[128,512]{0,1:T(8,128)(2,1)S(1)} %copy.95), channel_id=1, source_target_pairs={{0,6},{2,8},{4,10},{6,12},{8,14},{10,16},{12,18},{14,20},{16,22},{... | collective-permute-start | bytes 393224 | tf_op jit(solution)/shard_map/ppermute | solution.py:18
  20.7 19.2 %collective-permute-start.1 = (bf16[128,512]{0,1:T(8,128)(2,1)S(1)}, bf16[128,512]{0,1:T(8,128)(2,1)S(1)}, u32[]{:S(2)}, u32[]{:S(2)}) collective-permute-start(bf16[128,512]{0,1:T(8,128)(2,1)S(1)} %copy.85), channel_id=1, source_target_pairs={{0,14},{2,16},{4,18},{6,20},{8,22},{10,24},{12,26},{14,28},{16,30}... | collective-permute-start | bytes 393224 | tf_op jit(solution)/shard_map/ppermute | solution.py:18
  24.7 11.0 %collective-permute-start = (bf16[128,512]{0,1:T(8,128)(2,1)S(1)}, bf16[128,512]{0,1:T(8,128)(2,1)S(1)}, u32[]{:S(2)}, u32[]{:S(2)}) collective-permute-start(bf16[128,512]{0,1:T(8,128)(2,1)S(1)} %copy.85), channel_id=1, source_target_pairs={{0,16},{2,18},{4,20},{6,22},{8,24},{10,26},{12,28},{14,30},{16,32}... | collective-permute-start | bytes 393224 | tf_op jit(solution)/shard_map/ppermute | solution.py:18
  35.7 11.9 %collective-permute-start.2 = (bf16[128,512]{0,1:T(8,128)(2,1)S(1)}, bf16[128,512]{0,1:T(8,128)(2,1)S(1)}, u32[]{:S(2)}, u32[]{:S(2)}) collective-permute-start(bf16[128,512]{0,1:T(8,128)(2,1)S(1)} %copy.85), channel_id=1, source_target_pairs={{0,12},{2,14},{4,16},{6,18},{8,20},{10,22},{12,24},{14,26},{16,28}... | collective-permute-start | bytes 393224 | tf_op jit(solution)/shard_map/ppermute | solution.py:18
  39.9 12.6 %collective-permute-start.3 = (bf16[128,512]{0,1:T(8,128)(2,1)S(1)}, bf16[128,512]{0,1:T(8,128)(2,1)S(1)}, u32[]{:S(2)}, u32[]{:S(2)}) collective-permute-start(bf16[128,512]{0,1:T(8,128)(2,1)S(1)} %copy.85), channel_id=1, source_target_pairs={{0,10},{2,12},{4,14},{6,16},{8,18},{10,20},{12,22},{14,24},{16,26}... | collective-permute-start | bytes 393224 | tf_op jit(solution)/shard_map/ppermute | solution.py:18
  66.6 17.2 %collective-permute-start.9 = (bf16[128,512]{0,1:T(8,128)(2,1)S(1)}, bf16[128,512]{0,1:T(8,128)(2,1)S(1)}, u32[]{:S(2)}, u32[]{:S(2)}) collective-permute-start(bf16[128,512]{0,1:T(8,128)(2,1)S(1)} %copy.95), channel_id=1, source_target_pairs={{0,14},{2,16},{4,18},{6,20},{8,22},{10,24},{12,26},{14,28},{16,30}... | collective-permute-start | bytes 393224 | tf_op jit(solution)/shard_map/ppermute | solution.py:18
  70.7 10.2 %collective-permute-start.8 = (bf16[128,512]{0,1:T(8,128)(2,1)S(1)}, bf16[128,512]{0,1:T(8,128)(2,1)S(1)}, u32[]{:S(2)}, u32[]{:S(2)}) collective-permute-start(bf16[128,512]{0,1:T(8,128)(2,1)S(1)} %copy.95), channel_id=1, source_target_pairs={{0,16},{2,18},{4,20},{6,22},{8,24},{10,26},{12,28},{14,30},{16,32}... | collective-permute-start | bytes 393224 | tf_op jit(solution)/shard_map/ppermute | solution.py:18
  83.8 10.4 %collective-permute-start.11 = (bf16[128,512]{0,1:T(8,128)(2,1)S(1)}, bf16[128,512]{0,1:T(8,128)(2,1)S(1)}, u32[]{:S(2)}, u32[]{:S(2)}) collective-permute-start(bf16[128,512]{0,1:T(8,128)(2,1)S(1)} %copy.95), channel_id=1, source_target_pairs={{0,10},{2,12},{4,14},{6,16},{8,18},{10,20},{12,22},{14,24},{16,26}... | collective-permute-start | bytes 393224 | tf_op jit(solution)/shard_map/ppermute | solution.py:18
  88.7 10.1 %collective-permute-start.12 = (bf16[128,512]{0,1:T(8,128)(2,1)S(1)}, bf16[128,512]{0,1:T(8,128)(2,1)S(1)}, u32[]{:S(2)}, u32[]{:S(2)}) collective-permute-start(bf16[128,512]{0,1:T(8,128)(2,1)S(1)} %copy.95), channel_id=1, source_target_pairs={{0,8},{2,10},{4,12},{6,14},{8,16},{10,18},{12,20},{14,22},{16,24},... | collective-permute-start | bytes 393224 | tf_op jit(solution)/shard_map/ppermute | solution.py:18
  294.2 77.7 %collective-permute-start.33 = (f32[1024,88]{0,1:T(8,128)S(1)}, f32[1024,88]{0,1:T(8,128)}, u32[]{:S(2)}, u32[]{:S(2)}) collective-permute-start(f32[1024,88]{0,1:T(8,128)S(1)} %fusion.4), channel_id=1, source_target_pairs={{0,4},{2,6},{4,8},{6,10},{8,12},{10,14},{12,16},{14,18},{16,20},{1... | collective-permute-start | bytes 1081352
  300.4 80.0 %collective-permute-start.32 = (f32[1024,88]{0,1:T(8,128)S(1)}, f32[1024,88]{0,1:T(8,128)}, u32[]{:S(2)}, u32[]{:S(2)}) collective-permute-start(f32[1024,88]{0,1:T(8,128)S(1)} %fusion.4), channel_id=1, source_target_pairs={{0,2},{2,4},{4,6},{6,8},{8,10},{10,12},{12,14},{14,16},{16,18},{18... | collective-permute-start | bytes 1081352
  305.8 64.1 %collective-permute-start.34 = (f32[1024,76]{0,1:T(8,128)}, f32[1024,76]{0,1:T(8,128)}, u32[]{:S(2)}, u32[]{:S(2)}) collective-permute-start(f32[1024,76]{0,1:T(8,128)} %slice.162), channel_id=1, source_target_pairs={{0,6},{2,8},{4,10},{6,12},{8,14},{10,16},{12,18},{14,20},{16,22},{... | collective-permute-start | bytes 933896
  363.3 19.0 %collective-permute-start.24 = (f32[128,512]{1,0:T(8,128)S(1)}, f32[128,512]{1,0:T(8,128)S(1)}, u32[]{:S(2)}, u32[]{:S(2)}) collective-permute-start(f32[128,512]{1,0:T(8,128)S(1)} %bitcast.311), channel_id=1, source_target_pairs={{2,0},{4,2},{6,4},{8,6},{10,8},{12,10},{14,12},{16,14},{18,16},{20... | collective-permute-start | bytes 786440 | tf_op jit(solution)/shard_map/ppermute | solution.py:18
  367.8 19.6 %collective-permute-start.25 = (f32[128,512]{1,0:T(8,128)S(1)}, f32[128,512]{1,0:T(8,128)S(1)}, u32[]{:S(2)}, u32[]{:S(2)}) collective-permute-start(f32[128,512]{1,0:T(8,128)S(1)} %bitcast.309), channel_id=1, source_target_pairs={{4,0},{6,2},{8,4},{10,6},{12,8},{14,10},{16,12},{18,14},{20,16},{2... | collective-permute-start | bytes 786440 | tf_op jit(solution)/shard_map/ppermute | solution.py:18
  369.9 22.8 %collective-permute-start.26 = (f32[128,512]{1,0:T(8,128)S(1)}, f32[128,512]{1,0:T(8,128)S(1)}, u32[]{:S(2)}, u32[]{:S(2)}) collective-permute-start(f32[128,512]{1,0:T(8,128)S(1)} %bitcast.307), channel_id=1, source_target_pairs={{6,0},{8,2},{10,4},{12,6},{14,8},{16,10},{18,12},{20,14},{22,16},{... | collective-permute-start | bytes 786440 | tf_op jit(solution)/shard_map/ppermute | solution.py:18
  371.8 32.1 %collective-permute-start.27 = (f32[128,512]{1,0:T(8,128)S(1)}, f32[128,512]{1,0:T(8,128)}, u32[]{:S(2)}, u32[]{:S(2)}) collective-permute-start(f32[128,512]{1,0:T(8,128)S(1)} %bitcast.304), channel_id=1, source_target_pairs={{8,0},{10,2},{12,4},{14,6},{16,8},{18,10},{20,12},{22,14},{24,16},... | collective-permute-start | bytes 786440 | tf_op jit(solution)/shard_map/ppermute | solution.py:18
  380.4 25.8 %collective-permute-start.28 = (f32[128,512]{1,0:T(8,128)S(1)}, f32[128,512]{1,0:T(8,128)}, u32[]{:S(2)}, u32[]{:S(2)}) collective-permute-start(f32[128,512]{1,0:T(8,128)S(1)} %bitcast.302), channel_id=1, source_target_pairs={{10,0},{12,2},{14,4},{16,6},{18,8},{20,10},{22,12},{24,14},{26,16}... | collective-permute-start | bytes 786440 | tf_op jit(solution)/shard_map/ppermute | solution.py:18
  382.4 25.8 %collective-permute-start.29 = (f32[128,512]{1,0:T(8,128)S(1)}, f32[128,512]{1,0:T(8,128)}, u32[]{:S(2)}, u32[]{:S(2)}) collective-permute-start(f32[128,512]{1,0:T(8,128)S(1)} %bitcast.301), channel_id=1, source_target_pairs={{12,0},{14,2},{16,4},{18,6},{20,8},{22,10},{24,12},{26,14},{28,16}... | collective-permute-start | bytes 786440 | tf_op jit(solution)/shard_map/ppermute | solution.py:18
  387.4 30.1 %collective-permute-start.30 = (f32[128,512]{1,0:T(8,128)}, f32[128,512]{1,0:T(8,128)}, u32[]{:S(2)}, u32[]{:S(2)}) collective-permute-start(f32[128,512]{1,0:T(8,128)} %bitcast.233), channel_id=1, source_target_pairs={{14,0},{16,2},{18,4},{20,6},{22,8},{24,10},{26,12},{28,14},{30,16}... | collective-permute-start | bytes 786440 | tf_op jit(solution)/shard_map/ppermute | solution.py:18
  392.7 30.2 %collective-permute-start.31 = (f32[128,512]{1,0:T(8,128)}, f32[128,512]{1,0:T(8,128)}, u32[]{:S(2)}, u32[]{:S(2)}) collective-permute-start(f32[128,512]{1,0:T(8,128)} %bitcast.232), channel_id=1, source_target_pairs={{16,0},{18,2},{20,4},{22,6},{24,8},{26,10},{28,12},{30,14},{32,16}... | collective-permute-start | bytes 786440 | tf_op jit(solution)/shard_map/ppermute | solution.py:18
  404.0 20.8 %collective-permute-start.16 = (f32[128,512]{1,0:T(8,128)}, f32[128,512]{1,0:T(8,128)}, u32[]{:S(2)}, u32[]{:S(2)}) collective-permute-start(f32[128,512]{1,0:T(8,128)} %bitcast.247), channel_id=1, source_target_pairs={{2,0},{4,2},{6,4},{8,6},{10,8},{12,10},{14,12},{16,14},{18,16},{20... | collective-permute-start | bytes 786440 | tf_op jit(solution)/shard_map/ppermute | solution.py:18
  406.2 20.5 %collective-permute-start.17 = (f32[128,512]{1,0:T(8,128)}, f32[128,512]{1,0:T(8,128)}, u32[]{:S(2)}, u32[]{:S(2)}) collective-permute-start(f32[128,512]{1,0:T(8,128)} %bitcast.246), channel_id=1, source_target_pairs={{4,0},{6,2},{8,4},{10,6},{12,8},{14,10},{16,12},{18,14},{20,16},{2... | collective-permute-start | bytes 786440 | tf_op jit(solution)/shard_map/ppermute | solution.py:18
  408.2 21.1 %collective-permute-start.18 = (f32[128,512]{1,0:T(8,128)}, f32[128,512]{1,0:T(8,128)}, u32[]{:S(2)}, u32[]{:S(2)}) collective-permute-start(f32[128,512]{1,0:T(8,128)} %bitcast.245), channel_id=1, source_target_pairs={{6,0},{8,2},{10,4},{12,6},{14,8},{16,10},{18,12},{20,14},{22,16},{... | collective-permute-start | bytes 786440 | tf_op jit(solution)/shard_map/ppermute | solution.py:18
  417.6 18.4 %collective-permute-start.19 = (f32[128,512]{1,0:T(8,128)S(1)}, f32[128,512]{1,0:T(8,128)S(1)}, u32[]{:S(2)}, u32[]{:S(2)}) collective-permute-start(f32[128,512]{1,0:T(8,128)S(1)} %bitcast.310), channel_id=1, source_target_pairs={{8,0},{10,2},{12,4},{14,6},{16,8},{18,10},{20,12},{22,14},{24,16},... | collective-permute-start | bytes 786440 | tf_op jit(solution)/shard_map/ppermute | solution.py:18
  422.9 19.4 %collective-permute-start.20 = (f32[128,512]{1,0:T(8,128)S(1)}, f32[128,512]{1,0:T(8,128)S(1)}, u32[]{:S(2)}, u32[]{:S(2)}) collective-permute-start(f32[128,512]{1,0:T(8,128)S(1)} %bitcast.308), channel_id=1, source_target_pairs={{10,0},{12,2},{14,4},{16,6},{18,8},{20,10},{22,12},{24,14},{26,16}... | collective-permute-start | bytes 786440 | tf_op jit(solution)/shard_map/ppermute | solution.py:18
  424.8 23.1 %collective-permute-start.21 = (f32[128,512]{1,0:T(8,128)S(1)}, f32[128,512]{1,0:T(8,128)S(1)}, u32[]{:S(2)}, u32[]{:S(2)}) collective-permute-start(f32[128,512]{1,0:T(8,128)S(1)} %bitcast.306), channel_id=1, source_target_pairs={{12,0},{14,2},{16,4},{18,6},{20,8},{22,10},{24,12},{26,14},{28,16}... | collective-permute-start | bytes 786440 | tf_op jit(solution)/shard_map/ppermute | solution.py:18
  426.8 26.8 %collective-permute-start.22 = (f32[128,512]{1,0:T(8,128)S(1)}, f32[128,512]{1,0:T(8,128)S(1)}, u32[]{:S(2)}, u32[]{:S(2)}) collective-permute-start(f32[128,512]{1,0:T(8,128)S(1)} %bitcast.305), channel_id=1, source_target_pairs={{14,0},{16,2},{18,4},{20,6},{22,8},{24,10},{26,12},{28,14},{30,16}... | collective-permute-start | bytes 786440 | tf_op jit(solution)/shard_map/ppermute | solution.py:18
  429.3 50.3 %collective-permute-start.23 = (f32[128,512]{1,0:T(8,128)S(1)}, f32[128,512]{1,0:T(8,128)S(1)}, u32[]{:S(2)}, u32[]{:S(2)}) collective-permute-start(f32[128,512]{1,0:T(8,128)S(1)} %bitcast.303), channel_id=1, source_target_pairs={{16,0},{18,2},{20,4},{22,6},{24,8},{26,10},{28,12},{30,14},{32,16}... | collective-permute-start | bytes 786440 | tf_op jit(solution)/shard_map/ppermute | solution.py:18
  (18 other events, 244.0 us)
Sparse Core Ops, SparseCore 0:
  9.6 30.4 all-gather.3
  41.8 153.8 all-gather.5
where the time goes:
time: 490 us; the launch traced here: 488 us
  blocking collectives  173 us (35%)
  starting transfers between devices  120 us (24%)
  waiting for transfers between devices  91.8 us (19%)
  matrix products  40.1 us (8%)
  local copies, waits for them, and re-layouts  35.9 us (7%)
  between operations  15.6 us (3%)
  other arithmetic  11.8 us (2%)
    unnamed x1, blocking collectives  173 us
    ppermute x32, starting transfers between devices, from_behind(): return lax.ppermute(block, axis, route)  98.1 us
    ppermute x32, waiting for transfers between devices, from_behind(): return lax.ppermute(block, axis, route)  91 us
    unnamed x54, local copies, waits for them, and re-layouts  28.8 us
    unnamed x3, starting transfers between devices  22.1 us
    dot_general x1, matrix products, per_device(): jnp.dot(attention_probs.T, cotangent, preferred_element_type=jnp.float32)  10.9 us
  transfers between devices with their start and end apart: 37, of which 19 were waited for; matrix products, arithmetic and copies ran while one was open for 53% of the time, Pallas kernels for 0%

commit v1 on v0

--- a/solution.py
+++ b/solution.py
@@ -61,15 +61,15 @@
 
 def per_device(rotated_queries, rotated_keys, value_matrix, out_grad, out_weight):
     tokens_dev = rotated_queries.shape[0]
-    n_ctx = lax.axis_size("ctx")
+    n_ctx = lax.axis_size(("cg", "cp"))
     kv_local = rotated_keys.shape[1] // HEAD_SIZE
     group_width = QUERY_HEAD_COUNT // KEY_VALUE_HEADS
     reach_count = WINDOW_SPAN // tokens_dev
-    start_pos = lax.axis_index("ctx") * tokens_dev
+    start_pos = lax.axis_index(("cg", "cp")) * tokens_dev
     query_pos = start_pos + jnp.arange(tokens_dev, dtype=jnp.int32)
     earlier = []
     for offset in range(reach_count, 0, -1):
-        earlier.append(from_behind((rotated_keys, value_matrix), "ctx", offset))
+        earlier.append(from_behind((rotated_keys, value_matrix), ("cg", "cp"), offset))
     key_ext = jnp.concatenate([pair[0] for pair in earlier] + [rotated_keys], 0)
     value_ext = jnp.concatenate([pair[1] for pair in earlier] + [value_matrix], 0)
     key_pos = (
@@ -92,15 +92,23 @@
     cotangent = lax.all_gather(out_grad, "tp", axis=1, tiled=True)
     grad_sum = lax.dot_general(
         cotangent,
-        lax.all_gather(out_weight, "ctx", axis=1, tiled=True),
+        lax.all_gather(out_weight, ("cg", "cp"), axis=1, tiled=True),
         (((1,), (1,)), ((), ())),
         preferred_element_type=jnp.float32,
     )
     attention_gradient = grad_sum.astype(jnp.bfloat16)
-    weight_term = jnp.dot(attention_probs.T, cotangent, preferred_element_type=jnp.float32) * (
-        tokens_dev * n_ctx
-    ) ** (-0.5)
-    weight_grad = lax.psum_scatter(weight_term, "ctx", scatter_dimension=1, tiled=True)
+    group_size = lax.axis_size("cp")
+    group_count = lax.axis_size("cg")
+    block = cotangent.shape[1] // n_ctx
+    by_position = cotangent.reshape(tokens_dev, group_count, group_size, block).transpose(0, 2, 1, 3)
+    group_cotangent = lax.all_to_all(by_position, "cp", 1, 0, tiled=True).reshape(
+        group_size * tokens_dev, group_count, block
+    )
+    group_probs = lax.all_gather(attention_probs, "cp", axis=0, tiled=True)
+    weight_term = jnp.einsum(
+        "th,tak->ahk", group_probs, group_cotangent, preferred_element_type=jnp.float32
+    ) * (tokens_dev * n_ctx) ** (-0.5)
+    weight_grad = lax.psum_scatter(weight_term, "cg", scatter_dimension=0, tiled=True)[0]
     grad_rows = attention_gradient.reshape(tokens_dev, kv_local, group_width, HEAD_SIZE)
     row_deltas = jnp.sum(grad_rows.astype(jnp.float32) * attn_rows.astype(jnp.float32), axis=-1)
     head_gradients = grad_rows.transpose(1, 0, 2, 3)
@@ -122,7 +130,7 @@
                 key_ext_grad[first_row : first_row + tokens_dev],
                 value_ext_grad[first_row : first_row + tokens_dev],
             ),
-            "ctx",
+            ("cg", "cp"),
             -offset,
         )
         key_total = key_total + back_key
@@ -136,12 +144,20 @@
     )
 
 
+GROUP_SIZE = 8
+
+
 def solution(mesh):
-    placed = (P("ctx", "tp"), P("ctx", "tp"), P("ctx", "tp"), P("ctx", "tp"), P("tp", "ctx"))
+    n_ctx = mesh.shape["ctx"]
+    group_size = GROUP_SIZE if n_ctx % GROUP_SIZE == 0 else 1
+    devices = mesh.devices.reshape(n_ctx // group_size, group_size, mesh.shape["tp"])
+    grouped = jax.sharding.Mesh(devices, ("cg", "cp", "tp"))
+    ctx = ("cg", "cp")
+    placed = (P(ctx, "tp"), P(ctx, "tp"), P(ctx, "tp"), P(ctx, "tp"), P("tp", ctx))
     return jax.shard_map(
         per_device,
-        mesh=mesh,
+        mesh=grouped,
         in_specs=placed,
-        out_specs=(P("ctx", "tp"), P("ctx", "tp"), P("ctx", "tp"), P("tp", "ctx")),
+        out_specs=(P(ctx, "tp"), P(ctx, "tp"), P(ctx, "tp"), P("tp", ctx)),
         check_vma=False,
     )

time: 490 us -> 438 us (0.89)
  blocking collectives: 173 us -> 0 us
  waiting for transfers between devices: 91.8 us -> 239 us
  starting transfers between devices: 120 us -> 91.8 us
  local copies, waits for them, and re-layouts: 35.9 us -> 43 us
  matrix products: 40.1 us -> 33.8 us
    unnamed x1 -> x0, blocking collectives: 173 us -> none
    all_gather x1 -> x2, waiting for transfers between devices: 0.02 us -> 101 us  [the longest x1 101 us: per_device(): lax.all_gather(out_weight, ('cg', 'cp'), axis=1, tiled=True)]
    all_to_all x0 -> x1, waiting for transfers between devices: none -> 25.7 us  [per_device(): lax.all_to_all(by_position, 'cp', 1, 0, tiled=True)]
    unnamed x3 -> x0, starting transfers between devices: 22.1 us -> none
    ppermute x32, waiting for transfers between devices: 91 us -> 112 us  [from_behind(): return lax.ppermute(block, axis, route)]
    ppermute x32, starting transfers between devices: 98.1 us -> 87.5 us  [from_behind(): return lax.ppermute(block, axis, route)]
    reshape x0 -> x4, local copies, waits for them, and re-layouts: none -> 9.26 us  [the longest x2 5.03 us: per_device(): lax.all_to_all(by_position, 'cp', 1, 0, tiled=True)]
    unnamed x54 -> x34, local copies, waits for them, and re-layouts: 28.8 us -> 21.7 us
  transfers between devices with their start and end apart: 37 -> 37, of which waited for: 19 -> 28; matrix products, arithmetic and copies ran while one was open for 53% -> 20% of each run, Pallas kernels for 0% -> 0%
where the time goes in v1:
time: 438 us; the launch traced here: 434 us
  waiting for transfers between devices  239 us (55%)
  starting transfers between devices  91.8 us (21%)
  local copies, waits for them, and re-layouts  43 us (10%)
  matrix products  33.8 us (8%)
  between operations  14.5 us (3%)
  other arithmetic  11.6 us (3%)
    ppermute x32, waiting for transfers between devices, from_behind(): return lax.ppermute(block, axis, route)  112 us
    all_gather x1, waiting for transfers between devices, per_device(): lax.all_gather(out_weight, ('cg', 'cp'), axis=1, tiled=True)  101 us
    ppermute x32, starting transfers between devices, from_behind(): return lax.ppermute(block, axis, route)  87.5 us
    all_to_all x1, waiting for transfers between devices, per_device(): lax.all_to_all(by_position, 'cp', 1, 0, tiled=True)  25.7 us
    unnamed x34, local copies, waits for them, and re-layouts  21.7 us
  transfers between devices with their start and end apart: 37, of which 28 were waited for; matrix products, arithmetic and copies ran while one was open for 20% of the time, Pallas kernels for 0%

profile of v1, /device:TPU:8, one launch (start us, length us, event | category | flops | bytes accessed | tf_op | source)
XLA Modules:
  0.0 434.1 jit_solution(8999162186961649120)
XLA Ops:
  10.2 3.8 collective-permute-start.14
  14.0 4.9 %collective-permute-start.13 = (bf16[128,512]{0,1:T(8,128)(2,1)S(1)}, bf16[128,512]{0,1:T(8,128)(2,1)S(1)}, u32[]{:S(2)}, u32[]{:S(2)}) collective-permute-start(bf16[128,512]{0,1:T(8,128)(2,1)S(1)} %copy.101), channel_id=1, source_target_pairs={{0,6},{2,8},{4,10},{6,12},{8,14},{10,16},{12,18},{14,20},{16,22},{... | collective-permute-start | bytes 393224 | tf_op jit(solution)/shard_map/ppermute | solution.py:18
  20.0 4.1 collective-permute-start.1
  38.6 4.4 %collective-permute-start.4 = (bf16[128,512]{0,1:T(8,128)(2,1)S(1)}, bf16[128,512]{0,1:T(8,128)(2,1)S(1)}, u32[]{:S(2)}, u32[]{:S(2)}) collective-permute-start(bf16[128,512]{0,1:T(8,128)(2,1)S(1)} %copy.91), channel_id=1, source_target_pairs={{0,8},{2,10},{4,12},{6,14},{8,16},{10,18},{12,20},{14,22},{16,24},... | collective-permute-start | bytes 393224 | tf_op jit(solution)/shard_map/ppermute | solution.py:18
  44.1 4.5 %collective-permute-start.5 = (bf16[128,512]{0,1:T(8,128)(2,1)S(1)}, bf16[128,512]{0,1:T(8,128)(2,1)S(1)}, u32[]{:S(2)}, u32[]{:S(2)}) collective-permute-start(bf16[128,512]{0,1:T(8,128)(2,1)S(1)} %copy.91), channel_id=1, source_target_pairs={{0,6},{2,8},{4,10},{6,12},{8,14},{10,16},{12,18},{14,20},{16,22},{... | collective-permute-start | bytes 393224 | tf_op jit(solution)/shard_map/ppermute | solution.py:18
  48.6 3.9 collective-permute-done.4
  61.2 4.5 %collective-permute-done.6 = bf16[128,512]{0,1:T(8,128)(2,1)S(1)} collective-permute-done((bf16[128,512]{0,1:T(8,128)(2,1)S(1)}, bf16[128,512]{0,1:T(8,128)(2,1)S(1)}, u32[]{:S(2)}, u32[]{:S(2)}) %collective-permute-start.6) | collective-permute-done | bytes 131104 | tf_op jit(solution)/shard_map/ppermute | solution.py:18
  70.3 4.7 %collective-permute-done.8 = bf16[128,512]{0,1:T(8,128)(2,1)S(1)} collective-permute-done((bf16[128,512]{0,1:T(8,128)(2,1)S(1)}, bf16[128,512]{0,1:T(8,128)(2,1)S(1)}, u32[]{:S(2)}, u32[]{:S(2)}) %collective-permute-start.8) | collective-permute-done | bytes 131104 | tf_op jit(solution)/shard_map/ppermute | solution.py:18
  79.2 3.5 collective-permute-done.10
  82.7 4.5 %collective-permute-start.12 = (bf16[128,512]{0,1:T(8,128)(2,1)S(1)}, bf16[128,512]{0,1:T(8,128)(2,1)S(1)}, u32[]{:S(2)}, u32[]{:S(2)}) collective-permute-start(bf16[128,512]{0,1:T(8,128)(2,1)S(1)} %copy.101), channel_id=1, source_target_pairs={{0,8},{2,10},{4,12},{6,14},{8,16},{10,18},{12,20},{14,22},{16,24},... | collective-permute-start | bytes 393224 | tf_op jit(solution)/shard_map/ppermute | solution.py:18
  87.4 4.6 %collective-permute-done.12 = bf16[128,512]{0,1:T(8,128)(2,1)S(1)} collective-permute-done((bf16[128,512]{0,1:T(8,128)(2,1)S(1)}, bf16[128,512]{0,1:T(8,128)(2,1)S(1)}, u32[]{:S(2)}, u32[]{:S(2)}) %collective-permute-start.12) | collective-permute-done | bytes 131104 | tf_op jit(solution)/shard_map/ppermute | solution.py:18
  94.8 7.3 %while.28 = (s32[]{:T(128)}, bf16[4,128,2,128]{1,3,2,0:T(8,128)(2,1)S(1)}, f32[4,2,128]{2,1,0:T(2,128)S(1)}, bf16[4,1152,128]{1,2,0:T(8,128)(2,1)S(1)}, bf16[4,1...) while((s32[]{:T(128)}, ...), condition=%wide.region_3.4_spmd.clone, body=%wide.region_0.3_spmd.clone.sunk | while | flops 153829120 | bytes 4571377 | solution.py:86
  113.0 3.9 all-to-all-start
  117.2 25.7 %all-to-all-done = bf16[128,8,8,84]{0,2,3,1:T(8,128)(2,1)S(1)} async-done(((bf16[128,8,8,84]{0,2,3,1:T(8,128)(2,1)}), bf16[128,8,8,84]{0,2,3,1:T(8,128)(2,1)S(1)}, u32[]{:S(2)}, u32[]{:S(2)}) %all-to-all-start) | async-done | bytes 1376288 | tf_op jit(solution)/shard_map/all_to_all | solution.py:104
  147.9 5.4 %multiply_bitcast_fusion = f32[8,1024,84]{1,2,0:T(8,128)} fusion(bf16[1024,8,84]{0,2,1:T(8,128)(2,1)} %reshape.112, bf16[1024,1024]{1,0:T(8,128)(2,1)} %all-gather.7.cloned.1.call-done), kind=kOutput, calls=%fused_computation.69 | convolution fusion | flops 1409974272 | bytes 6225920 | tf_op jit(solution)/shard_map/th,tak->ahk/dot_general | solution.py:108
  153.3 100.9 %all-gather.9.cloned.1.call-done = bf16[64,84,1024]{2,1,0:T(8,128)(2,1)} async-done(((bf16[1,84,1024]{2,1,0:T(8,128)(2,1)}), bf16[64,84,1024]{2,1,0:T(8,128)(2,1)}) %all-gather.9.cloned.1.call-update) | async-done | bytes 11010064 | tf_op jit(solution)/shard_map/all_gather | solution.py:95
  254.2 14.1 %reshape.103 = bf16[5376,1024]{1,0:T(8,128)(2,1)} reshape(bf16[64,84,1024]{2,1,0:T(8,128)(2,1)} %all-gather.9.cloned.1.call-done) | data formatting | bytes 22020096
  268.4 5.7 %convolution_convert_fusion.1 = bf16[128,1024]{1,0:T(8,128)(2,1)S(1)} fusion(bf16[128,5376]{1,0:T(8,128)(2,1)S(1)} %copy-done, bf16[5376,1024]{1,0:T(8,128)(2,1)} %reshape.103), kind=kOutput, calls=%fused_computation.72 | convolution fusion | flops 1409417216 | bytes 12648448 | tf_op jit(solution)/shard_map/dot_general | solution.py:93
  274.6 23.3 %while.29 = (s32[]{:T(128)}, bf16[4,128,2,128]{1,3,2,0:T(8,128)(2,1)}, f32[4,1152,128]{2,1,0:T(8,128)}, f32[4,1152,128]{2,1,0:T(8,128)}, bf16[4,1152,128]{2,1,0:...) while((s32[]{:T(128)}, ...), condition=%wide.region_6.7_spmd.clone, body=%wide.region_5.6_spmd.clone.sunk | while | flops 380469248 | bytes 8078613 | solution.py:116
  299.7 3.7 collective-permute-start.24
  315.3 7.7 %collective-permute-done.24 = f32[128,512]{1,0:T(8,128)S(1)} collective-permute-done((f32[128,512]{1,0:T(8,128)S(1)}, f32[128,512]{1,0:T(8,128)S(1)}, u32[]{:S(2)}, u32[]{:S(2)}) %collective-permute-start.24) | collective-permute-done | bytes 262176 | tf_op jit(solution)/shard_map/ppermute | solution.py:18
  327.5 7.2 %collective-permute-done.25 = f32[128,512]{1,0:T(8,128)S(1)} collective-permute-done((f32[128,512]{1,0:T(8,128)S(1)}, f32[128,512]{1,0:T(8,128)S(1)}, u32[]{:S(2)}, u32[]{:S(2)}) %collective-permute-start.25) | collective-permute-done | bytes 262176 | tf_op jit(solution)/shard_map/ppermute | solution.py:18
  336.5 6.5 %collective-permute-done.26 = f32[128,512]{1,0:T(8,128)S(1)} collective-permute-done((f32[128,512]{1,0:T(8,128)S(1)}, f32[128,512]{1,0:T(8,128)S(1)}, u32[]{:S(2)}, u32[]{:S(2)}) %collective-permute-start.26) | collective-permute-done | bytes 262176 | tf_op jit(solution)/shard_map/ppermute | solution.py:18
  344.9 8.2 %collective-permute-done.27 = f32[128,512]{1,0:T(8,128)S(1)} collective-permute-done((f32[128,512]{1,0:T(8,128)S(1)}, f32[128,512]{1,0:T(8,128)S(1)}, u32[]{:S(2)}, u32[]{:S(2)}) %collective-permute-start.27) | collective-permute-done | bytes 262176 | tf_op jit(solution)/shard_map/ppermute | solution.py:18
  355.1 4.5 %collective-permute-done.28 = f32[128,512]{1,0:T(8,128)S(1)} collective-permute-done((f32[128,512]{1,0:T(8,128)S(1)}, f32[128,512]{1,0:T(8,128)S(1)}, u32[]{:S(2)}, u32[]{:S(2)}) %collective-permute-start.28) | collective-permute-done | bytes 262176 | tf_op jit(solution)/shard_map/ppermute | solution.py:18
  361.5 3.7 collective-permute-done.29
  372.8 3.7 collective-permute-done.31
  378.4 10.3 %collective-permute-done.16 = f32[128,512]{1,0:T(8,128)} collective-permute-done((f32[128,512]{1,0:T(8,128)}, f32[128,512]{1,0:T(8,128)}, u32[]{:S(2)}, u32[]{:S(2)}) %collective-permute-start.16) | collective-permute-done | bytes 262176 | tf_op jit(solution)/shard_map/ppermute | solution.py:18
  390.7 3.7 collective-permute-done.17
  396.3 6.5 %collective-permute-done.18 = f32[128,512]{1,0:T(8,128)} collective-permute-done((f32[128,512]{1,0:T(8,128)}, f32[128,512]{1,0:T(8,128)}, u32[]{:S(2)}, u32[]{:S(2)}) %collective-permute-start.18) | collective-permute-done | bytes 262176 | tf_op jit(solution)/shard_map/ppermute | solution.py:18
  408.3 5.6 %collective-permute-done.20 = f32[128,512]{1,0:T(8,128)S(1)} collective-permute-done((f32[128,512]{1,0:T(8,128)S(1)}, f32[128,512]{1,0:T(8,128)S(1)}, u32[]{:S(2)}, u32[]{:S(2)}) %collective-permute-start.20) | collective-permute-done | bytes 262176 | tf_op jit(solution)/shard_map/ppermute | solution.py:18
  413.9 5.6 %collective-permute-done.21 = f32[128,512]{1,0:T(8,128)S(1)} collective-permute-done((f32[128,512]{1,0:T(8,128)S(1)}, f32[128,512]{1,0:T(8,128)S(1)}, u32[]{:S(2)}, u32[]{:S(2)}) %collective-permute-start.21) | collective-permute-done | bytes 262176 | tf_op jit(solution)/shard_map/ppermute | solution.py:18
  (175 shorter events, 139.3 us)
Async XLA Ops:
  7.2 96.8 %all-gather.5.cloned.1.call-start = ((), (), s32[]{:S(2)}) async-start(), calls=%async_computation.2 | async-start | bytes 2064384 | tf_op jit(solution)/shard_map/all_gather | solution.py:92
  8.3 86.5 %collective-permute-start.15 = (bf16[128,512]{0,1:T(8,128)(2,1)S(1)}, bf16[128,512]{0,1:T(8,128)(2,1)S(1)}, u32[]{:S(2)}, u32[]{:S(2)}) collective-permute-start(bf16[128,512]{0,1:T(8,128)(2,1)S(1)} %copy.101), channel_id=1, source_target_pairs={{0,2},{2,4},{4,6},{6,8},{8,10},{10,12},{12,14},{14,16},{16,18},{18... | collective-permute-start | bytes 393224 | tf_op jit(solution)/shard_map/ppermute | solution.py:18
  10.2 83.6 %collective-permute-start.14 = (bf16[128,512]{0,1:T(8,128)(2,1)S(1)}, bf16[128,512]{0,1:T(8,128)(2,1)}, u32[]{:S(2)}, u32[]{:S(2)}) collective-permute-start(bf16[128,512]{0,1:T(8,128)(2,1)S(1)} %copy.101), channel_id=1, source_target_pairs={{0,4},{2,6},{4,8},{6,10},{8,12},{10,14},{12,16},{14,18},{16,20},{1... | collective-permute-start | bytes 393224 | tf_op jit(solution)/shard_map/ppermute | solution.py:18
  14.0 78.0 %collective-permute-start.13 = (bf16[128,512]{0,1:T(8,128)(2,1)S(1)}, bf16[128,512]{0,1:T(8,128)(2,1)S(1)}, u32[]{:S(2)}, u32[]{:S(2)}) collective-permute-start(bf16[128,512]{0,1:T(8,128)(2,1)S(1)} %copy.101), channel_id=1, source_target_pairs={{0,6},{2,8},{4,10},{6,12},{8,14},{10,16},{12,18},{14,20},{16,22},{... | collective-permute-start | bytes 393224 | tf_op jit(solution)/shard_map/ppermute | solution.py:18
  20.0 14.3 %collective-permute-start.1 = (bf16[128,512]{0,1:T(8,128)(2,1)S(1)}, bf16[128,512]{0,1:T(8,128)(2,1)S(1)}, u32[]{:S(2)}, u32[]{:S(2)}) collective-permute-start(bf16[128,512]{0,1:T(8,128)(2,1)S(1)} %copy.91), channel_id=1, source_target_pairs={{0,14},{2,16},{4,18},{6,20},{8,22},{10,24},{12,26},{14,28},{16,30}... | collective-permute-start | bytes 393224 | tf_op jit(solution)/shard_map/ppermute | solution.py:18
  27.5 120.4 %all-gather.7.cloned.1.call-start = ((), (), s32[]{:S(2)}) async-start(), calls=%async_computation.3 | async-start | bytes 2359296 | tf_op jit(solution)/shard_map/all_gather | solution.py:107
  34.3 9.8 %collective-permute-start.3 = (bf16[128,512]{0,1:T(8,128)(2,1)S(1)}, bf16[128,512]{0,1:T(8,128)(2,1)S(1)}, u32[]{:S(2)}, u32[]{:S(2)}) collective-permute-start(bf16[128,512]{0,1:T(8,128)(2,1)S(1)} %copy.91), channel_id=1, source_target_pairs={{0,10},{2,12},{4,14},{6,16},{8,18},{10,20},{12,22},{14,24},{16,26}... | collective-permute-start | bytes 393224 | tf_op jit(solution)/shard_map/ppermute | solution.py:18
  38.6 13.9 %collective-permute-start.4 = (bf16[128,512]{0,1:T(8,128)(2,1)S(1)}, bf16[128,512]{0,1:T(8,128)(2,1)S(1)}, u32[]{:S(2)}, u32[]{:S(2)}) collective-permute-start(bf16[128,512]{0,1:T(8,128)(2,1)S(1)} %copy.91), channel_id=1, source_target_pairs={{0,8},{2,10},{4,12},{6,14},{8,16},{10,18},{12,20},{14,22},{16,24},... | collective-permute-start | bytes 393224 | tf_op jit(solution)/shard_map/ppermute | solution.py:18
  44.1 13.6 %collective-permute-start.5 = (bf16[128,512]{0,1:T(8,128)(2,1)S(1)}, bf16[128,512]{0,1:T(8,128)(2,1)S(1)}, u32[]{:S(2)}, u32[]{:S(2)}) collective-permute-start(bf16[128,512]{0,1:T(8,128)(2,1)S(1)} %copy.91), channel_id=1, source_target_pairs={{0,6},{2,8},{4,10},{6,12},{8,14},{10,16},{12,18},{14,20},{16,22},{... | collective-permute-start | bytes 393224 | tf_op jit(solution)/shard_map/ppermute | solution.py:18
  52.5 13.2 %collective-permute-start.6 = (bf16[128,512]{0,1:T(8,128)(2,1)S(1)}, bf16[128,512]{0,1:T(8,128)(2,1)S(1)}, u32[]{:S(2)}, u32[]{:S(2)}) collective-permute-start(bf16[128,512]{0,1:T(8,128)(2,1)S(1)} %copy.91), channel_id=1, source_target_pairs={{0,4},{2,6},{4,8},{6,10},{8,12},{10,14},{12,16},{14,18},{16,20},{1... | collective-permute-start | bytes 393224 | tf_op jit(solution)/shard_map/ppermute | solution.py:18
  57.7 10.3 %collective-permute-start.7 = (bf16[128,512]{0,1:T(8,128)(2,1)S(1)}, bf16[128,512]{0,1:T(8,128)(2,1)S(1)}, u32[]{:S(2)}, u32[]{:S(2)}) collective-permute-start(bf16[128,512]{0,1:T(8,128)(2,1)S(1)} %copy.91), channel_id=1, source_target_pairs={{0,2},{2,4},{4,6},{6,8},{8,10},{10,12},{12,14},{14,16},{16,18},{18... | collective-permute-start | bytes 393224 | tf_op jit(solution)/shard_map/ppermute | solution.py:18
  65.7 11.2 %collective-permute-start.9 = (bf16[128,512]{0,1:T(8,128)(2,1)S(1)}, bf16[128,512]{0,1:T(8,128)(2,1)S(1)}, u32[]{:S(2)}, u32[]{:S(2)}) collective-permute-start(bf16[128,512]{0,1:T(8,128)(2,1)S(1)} %copy.101), channel_id=1, source_target_pairs={{0,14},{2,16},{4,18},{6,20},{8,22},{10,24},{12,26},{14,28},{16,30}... | collective-permute-start | bytes 393224 | tf_op jit(solution)/shard_map/ppermute | solution.py:18
  76.9 10.4 %collective-permute-start.11 = (bf16[128,512]{0,1:T(8,128)(2,1)S(1)}, bf16[128,512]{0,1:T(8,128)(2,1)S(1)}, u32[]{:S(2)}, u32[]{:S(2)}) collective-permute-start(bf16[128,512]{0,1:T(8,128)(2,1)S(1)} %copy.101), channel_id=1, source_target_pairs={{0,10},{2,12},{4,14},{6,16},{8,18},{10,20},{12,22},{14,24},{16,26}... | collective-permute-start | bytes 393224 | tf_op jit(solution)/shard_map/ppermute | solution.py:18
  103.2 151.0 %all-gather.9.cloned.1.call-start = ((), (), s32[]{:S(2)}) async-start(), calls=%async_computation.5 | async-start | bytes 11714560 | tf_op jit(solution)/shard_map/all_gather | solution.py:95
  113.0 29.8 %all-to-all-start = ((bf16[128,8,8,84]{0,2,3,1:T(8,128)(2,1)}), bf16[128,8,8,84]{0,2,3,1:T(8,128)(2,1)S(1)}, u32[]{:S(2)}, u32[]{:S(2)}) async-start(bf16[128,8,8,84]{0,2,3,1:T(8,128)(2,1)} %copy.138), calls=%async_computation | async-start | bytes 2752512 | tf_op jit(solution)/shard_map/all_to_all | solution.py:104
  116.9 310.6 %reduce-scatter.2.cloned.1.call-start = ((), (), s32[]{:S(2)}) async-start(), calls=%async_computation.4 | async-start | bytes 3244032 | tf_op jit(solution)/shard_map/reduce_scatter | solution.py:111
  299.7 23.4 %collective-permute-start.24 = (f32[128,512]{1,0:T(8,128)S(1)}, f32[128,512]{1,0:T(8,128)S(1)}, u32[]{:S(2)}, u32[]{:S(2)}) collective-permute-start(f32[128,512]{1,0:T(8,128)S(1)} %bitcast.327), channel_id=1, source_target_pairs={{2,0},{4,2},{6,4},{8,6},{10,8},{12,10},{14,12},{16,14},{18,16},{20... | collective-permute-start | bytes 786440 | tf_op jit(solution)/shard_map/ppermute | solution.py:18
  305.0 29.6 %collective-permute-start.25 = (f32[128,512]{1,0:T(8,128)S(1)}, f32[128,512]{1,0:T(8,128)S(1)}, u32[]{:S(2)}, u32[]{:S(2)}) collective-permute-start(f32[128,512]{1,0:T(8,128)S(1)} %bitcast.326), channel_id=1, source_target_pairs={{4,0},{6,2},{8,4},{10,6},{12,8},{14,10},{16,12},{18,14},{20,16},{2... | collective-permute-start | bytes 786440 | tf_op jit(solution)/shard_map/ppermute | solution.py:18
  307.9 35.1 %collective-permute-start.26 = (f32[128,512]{1,0:T(8,128)S(1)}, f32[128,512]{1,0:T(8,128)S(1)}, u32[]{:S(2)}, u32[]{:S(2)}) collective-permute-start(f32[128,512]{1,0:T(8,128)S(1)} %bitcast.323), channel_id=1, source_target_pairs={{6,0},{8,2},{10,4},{12,6},{14,8},{16,10},{18,12},{20,14},{22,16},{... | collective-permute-start | bytes 786440 | tf_op jit(solution)/shard_map/ppermute | solution.py:18
  310.3 42.9 %collective-permute-start.27 = (f32[128,512]{1,0:T(8,128)S(1)}, f32[128,512]{1,0:T(8,128)S(1)}, u32[]{:S(2)}, u32[]{:S(2)}) collective-permute-start(f32[128,512]{1,0:T(8,128)S(1)} %bitcast.321), channel_id=1, source_target_pairs={{8,0},{10,2},{12,4},{14,6},{16,8},{18,10},{20,12},{22,14},{24,16},... | collective-permute-start | bytes 786440 | tf_op jit(solution)/shard_map/ppermute | solution.py:18
  313.4 46.2 %collective-permute-start.28 = (f32[128,512]{1,0:T(8,128)S(1)}, f32[128,512]{1,0:T(8,128)S(1)}, u32[]{:S(2)}, u32[]{:S(2)}) collective-permute-start(f32[128,512]{1,0:T(8,128)S(1)} %bitcast.318), channel_id=1, source_target_pairs={{10,0},{12,2},{14,4},{16,6},{18,8},{20,10},{22,12},{24,14},{26,16}... | collective-permute-start | bytes 786440 | tf_op jit(solution)/shard_map/ppermute | solution.py:18
  323.1 42.1 %collective-permute-start.29 = (f32[128,512]{1,0:T(8,128)S(1)}, f32[128,512]{1,0:T(8,128)S(1)}, u32[]{:S(2)}, u32[]{:S(2)}) collective-permute-start(f32[128,512]{1,0:T(8,128)S(1)} %bitcast.316), channel_id=1, source_target_pairs={{12,0},{14,2},{16,4},{18,6},{20,8},{22,10},{24,12},{26,14},{28,16}... | collective-permute-start | bytes 786440 | tf_op jit(solution)/shard_map/ppermute | solution.py:18
  334.6 36.3 %collective-permute-start.30 = (f32[128,512]{1,0:T(8,128)}, f32[128,512]{1,0:T(8,128)}, u32[]{:S(2)}, u32[]{:S(2)}) collective-permute-start(f32[128,512]{1,0:T(8,128)} %bitcast.247), channel_id=1, source_target_pairs={{14,0},{16,2},{18,4},{20,6},{22,8},{24,10},{26,12},{28,14},{30,16}... | collective-permute-start | bytes 786440 | tf_op jit(solution)/shard_map/ppermute | solution.py:18
  343.0 33.5 %collective-permute-start.31 = (f32[128,512]{1,0:T(8,128)}, f32[128,512]{1,0:T(8,128)}, u32[]{:S(2)}, u32[]{:S(2)}) collective-permute-start(f32[128,512]{1,0:T(8,128)} %bitcast.246), channel_id=1, source_target_pairs={{16,0},{18,2},{20,4},{22,6},{24,8},{26,10},{28,12},{30,14},{32,16}... | collective-permute-start | bytes 786440 | tf_op jit(solution)/shard_map/ppermute | solution.py:18
  353.2 35.6 %collective-permute-start.16 = (f32[128,512]{1,0:T(8,128)}, f32[128,512]{1,0:T(8,128)}, u32[]{:S(2)}, u32[]{:S(2)}) collective-permute-start(f32[128,512]{1,0:T(8,128)} %bitcast.261), channel_id=1, source_target_pairs={{2,0},{4,2},{6,4},{8,6},{10,8},{12,10},{14,12},{16,14},{18,16},{20... | collective-permute-start | bytes 786440 | tf_op jit(solution)/shard_map/ppermute | solution.py:18
  359.6 34.8 %collective-permute-start.17 = (f32[128,512]{1,0:T(8,128)}, f32[128,512]{1,0:T(8,128)}, u32[]{:S(2)}, u32[]{:S(2)}) collective-permute-start(f32[128,512]{1,0:T(8,128)} %bitcast.260), channel_id=1, source_target_pairs={{4,0},{6,2},{8,4},{10,6},{12,8},{14,10},{16,12},{18,14},{20,16},{2... | collective-permute-start | bytes 786440 | tf_op jit(solution)/shard_map/ppermute | solution.py:18
  365.2 37.6 %collective-permute-start.18 = (f32[128,512]{1,0:T(8,128)}, f32[128,512]{1,0:T(8,128)}, u32[]{:S(2)}, u32[]{:S(2)}) collective-permute-start(f32[128,512]{1,0:T(8,128)} %bitcast.259), channel_id=1, source_target_pairs={{6,0},{8,2},{10,4},{12,6},{14,8},{16,10},{18,12},{20,14},{22,16},{... | collective-permute-start | bytes 786440 | tf_op jit(solution)/shard_map/ppermute | solution.py:18
  370.9 37.4 %collective-permute-start.19 = (f32[128,512]{1,0:T(8,128)S(1)}, f32[128,512]{1,0:T(8,128)S(1)}, u32[]{:S(2)}, u32[]{:S(2)}) collective-permute-start(f32[128,512]{1,0:T(8,128)S(1)} %bitcast.324), channel_id=1, source_target_pairs={{8,0},{10,2},{12,4},{14,6},{16,8},{18,10},{20,12},{22,14},{24,16},... | collective-permute-start | bytes 786440 | tf_op jit(solution)/shard_map/ppermute | solution.py:18
  376.5 37.4 %collective-permute-start.20 = (f32[128,512]{1,0:T(8,128)S(1)}, f32[128,512]{1,0:T(8,128)S(1)}, u32[]{:S(2)}, u32[]{:S(2)}) collective-permute-start(f32[128,512]{1,0:T(8,128)S(1)} %bitcast.322), channel_id=1, source_target_pairs={{10,0},{12,2},{14,4},{16,6},{18,8},{20,10},{22,12},{24,14},{26,16}... | collective-permute-start | bytes 786440 | tf_op jit(solution)/shard_map/ppermute | solution.py:18
  388.8 30.7 %collective-permute-start.21 = (f32[128,512]{1,0:T(8,128)S(1)}, f32[128,512]{1,0:T(8,128)S(1)}, u32[]{:S(2)}, u32[]{:S(2)}) collective-permute-start(f32[128,512]{1,0:T(8,128)S(1)} %bitcast.320), channel_id=1, source_target_pairs={{12,0},{14,2},{16,4},{18,6},{20,8},{22,10},{24,12},{26,14},{28,16}... | collective-permute-start | bytes 786440 | tf_op jit(solution)/shard_map/ppermute | solution.py:18
  394.4 28.4 %collective-permute-start.22 = (f32[128,512]{1,0:T(8,128)S(1)}, f32[128,512]{1,0:T(8,128)S(1)}, u32[]{:S(2)}, u32[]{:S(2)}) collective-permute-start(f32[128,512]{1,0:T(8,128)S(1)} %bitcast.319), channel_id=1, source_target_pairs={{14,0},{16,2},{18,4},{20,6},{22,8},{24,10},{26,12},{28,14},{30,16}... | collective-permute-start | bytes 786440 | tf_op jit(solution)/shard_map/ppermute | solution.py:18
  402.8 22.8 %collective-permute-start.23 = (f32[128,512]{1,0:T(8,128)S(1)}, f32[128,512]{1,0:T(8,128)S(1)}, u32[]{:S(2)}, u32[]{:S(2)}) collective-permute-start(f32[128,512]{1,0:T(8,128)S(1)} %bitcast.317), channel_id=1, source_target_pairs={{16,0},{18,2},{20,4},{22,6},{24,8},{26,10},{28,12},{30,14},{32,16}... | collective-permute-start | bytes 786440 | tf_op jit(solution)/shard_map/ppermute | solution.py:18
  (10 other events, 119.4 us)
Sparse Core Ops, SparseCore 0:
  27.7 27.1 all-gather.4
  103.3 35.3 all-gather.6
  140.5 113.7 all-gather.8
  257.1 114.7 reduce-scatter.1

commit v2 on v1

--- a/solution.py
+++ b/solution.py
@@ -89,7 +89,12 @@
     )
     attn_rows = attn_heads.transpose(1, 0, 2, 3)
     attention_probs = attn_rows.reshape(tokens_dev, -1)
-    cotangent = lax.all_gather(out_grad, "tp", axis=1, tiled=True)
+    partner_grad = lax.ppermute(out_grad, "tp", [(0, 1), (1, 0)])
+    cotangent = jnp.where(
+        lax.axis_index("tp") == 0,
+        jnp.concatenate([out_grad, partner_grad], 1),
+        jnp.concatenate([partner_grad, out_grad], 1),
+    )
     grad_sum = lax.dot_general(
         cotangent,
         lax.all_gather(out_weight, ("cg", "cp"), axis=1, tiled=True),
@@ -100,11 +105,20 @@
     group_size = lax.axis_size("cp")
     group_count = lax.axis_size("cg")
     block = cotangent.shape[1] // n_ctx
-    by_position = cotangent.reshape(tokens_dev, group_count, group_size, block).transpose(0, 2, 1, 3)
-    group_cotangent = lax.all_to_all(by_position, "cp", 1, 0, tiled=True).reshape(
+    by_position = cotangent.reshape(tokens_dev, group_count, group_size, block).transpose(2, 0, 1, 3)
+    heads_width = attention_probs.shape[1]
+    outgoing = jnp.concatenate(
+        [
+            jnp.broadcast_to(attention_probs, (group_size,) + attention_probs.shape),
+            by_position.reshape(group_size, tokens_dev, group_count * block),
+        ],
+        2,
+    )
+    incoming = lax.all_to_all(outgoing, "cp", 0, 0, tiled=True)
+    group_probs = incoming[:, :, :heads_width].reshape(group_size * tokens_dev, heads_width)
+    group_cotangent = incoming[:, :, heads_width:].reshape(
         group_size * tokens_dev, group_count, block
     )
-    group_probs = lax.all_gather(attention_probs, "cp", axis=0, tiled=True)
     weight_term = jnp.einsum(
         "th,tak->ahk", group_probs, group_cotangent, preferred_element_type=jnp.float32
     ) * (tokens_dev * n_ctx) ** (-0.5)

time: 438 us -> 384 us (0.88)
  the two profiles are of different devices: /device:TPU:8 before, /device:TPU:6 now
where the time goes in v2:
time: 384 us; the launch traced here: 382 us
  waiting for transfers between devices  149 us (39%)
  starting transfers between devices  114 us (30%)
  local copies, waits for them, and re-layouts  48.1 us (13%)
  matrix products  37.1 us (10%)
  other arithmetic  17.3 us (5%)
  between operations  16.3 us (4%)
    ppermute x32, starting transfers between devices, from_behind(): return lax.ppermute(block, axis, route)  102 us
    ppermute x32, waiting for transfers between devices, from_behind(): return lax.ppermute(block, axis, route)  98.2 us
    all_to_all x1, waiting for transfers between devices, per_device(): incoming = lax.all_to_all(outgoing, 'cp', 0, 0, tiled=True)  41.8 us
    unnamed x35, local copies, waits for them, and re-layouts  26.1 us
    ppermute x1, waiting for transfers between devices, per_device(): partner_grad = lax.ppermute(out_grad, 'tp', [(0, 1), (1, 0)])  8.12 us
  transfers between devices with their start and end apart: 36, of which 22 were waited for; matrix products, arithmetic and copies ran while one was open for 27% of the time, Pallas kernels for 0%

profile of v2, /device:TPU:6, one launch (start us, length us, event | category | flops | bytes accessed | tf_op | source)
XLA Modules:
  0.0 381.5 jit_solution(1431042316034872800)
XLA Ops:
  11.7 3.8 %collective-permute-start.14 = (bf16[128,512]{0,1:T(8,128)(2,1)S(1)}, bf16[128,512]{0,1:T(8,128)(2,1)}, u32[]{:S(2)}, u32[]{:S(2)}) collective-permute-start(bf16[128,512]{0,1:T(8,128)(2,1)S(1)} %copy.102), channel_id=1, source_target_pairs={{0,4},{2,6},{4,8},{6,10},{8,12},{10,14},{12,16},{14,18},{16,20},{1... | collective-permute-start | bytes 393224 | tf_op jit(solution)/shard_map/ppermute | solution.py:18
  15.5 4.9 %collective-permute-start.13 = (bf16[128,512]{0,1:T(8,128)(2,1)S(1)}, bf16[128,512]{0,1:T(8,128)(2,1)S(1)}, u32[]{:S(2)}, u32[]{:S(2)}) collective-permute-start(bf16[128,512]{0,1:T(8,128)(2,1)S(1)} %copy.102), channel_id=1, source_target_pairs={{0,6},{2,8},{4,10},{6,12},{8,14},{10,16},{12,18},{14,20},{16,22},{... | collective-permute-start | bytes 393224 | tf_op jit(solution)/shard_map/ppermute | solution.py:18
  21.4 4.3 %collective-permute-start.1 = (bf16[128,512]{0,1:T(8,128)(2,1)S(1)}, bf16[128,512]{0,1:T(8,128)(2,1)S(1)}, u32[]{:S(2)}, u32[]{:S(2)}) collective-permute-start(bf16[128,512]{0,1:T(8,128)(2,1)S(1)} %copy.92), channel_id=1, source_target_pairs={{0,14},{2,16},{4,18},{6,20},{8,22},{10,24},{12,26},{14,28},{16,30}... | collective-permute-start | bytes 393224 | tf_op jit(solution)/shard_map/ppermute | solution.py:18
  30.6 6.2 %collective-permute-done = bf16[128,512]{0,1:T(8,128)(2,1)S(1)} collective-permute-done((bf16[128,512]{0,1:T(8,128)(2,1)S(1)}, bf16[128,512]{0,1:T(8,128)(2,1)S(1)}, u32[]{:S(2)}, u32[]{:S(2)}) %collective-permute-start) | collective-permute-done | bytes 131104 | tf_op jit(solution)/shard_map/ppermute | solution.py:18
  36.9 5.8 %collective-permute-start.2 = (bf16[128,512]{0,1:T(8,128)(2,1)S(1)}, bf16[128,512]{0,1:T(8,128)(2,1)S(1)}, u32[]{:S(2)}, u32[]{:S(2)}) collective-permute-start(bf16[128,512]{0,1:T(8,128)(2,1)S(1)} %copy.92), channel_id=1, source_target_pairs={{0,12},{2,14},{4,16},{6,18},{8,20},{10,22},{12,24},{14,26},{16,28}... | collective-permute-start | bytes 393224 | tf_op jit(solution)/shard_map/ppermute | solution.py:18
  44.7 3.7 collective-permute-done.2
  48.4 5.4 %collective-permute-start.4 = (bf16[128,512]{0,1:T(8,128)(2,1)S(1)}, bf16[128,512]{0,1:T(8,128)(2,1)S(1)}, u32[]{:S(2)}, u32[]{:S(2)}) collective-permute-start(bf16[128,512]{0,1:T(8,128)(2,1)S(1)} %copy.92), channel_id=1, source_target_pairs={{0,8},{2,10},{4,12},{6,14},{8,16},{10,18},{12,20},{14,22},{16,24},... | collective-permute-start | bytes 393224 | tf_op jit(solution)/shard_map/ppermute | solution.py:18
  53.9 4.4 %collective-permute-start.5 = (bf16[128,512]{0,1:T(8,128)(2,1)S(1)}, bf16[128,512]{0,1:T(8,128)(2,1)S(1)}, u32[]{:S(2)}, u32[]{:S(2)}) collective-permute-start(bf16[128,512]{0,1:T(8,128)(2,1)S(1)} %copy.92), channel_id=1, source_target_pairs={{0,6},{2,8},{4,10},{6,12},{8,14},{10,16},{12,18},{14,20},{16,22},{... | collective-permute-start | bytes 393224 | tf_op jit(solution)/shard_map/ppermute | solution.py:18
  59.3 5.7 %collective-permute-start.6 = (bf16[128,512]{0,1:T(8,128)(2,1)S(1)}, bf16[128,512]{0,1:T(8,128)(2,1)S(1)}, u32[]{:S(2)}, u32[]{:S(2)}) collective-permute-start(bf16[128,512]{0,1:T(8,128)(2,1)S(1)} %copy.92), channel_id=1, source_target_pairs={{0,4},{2,6},{4,8},{6,10},{8,12},{10,14},{12,16},{14,18},{16,20},{1... | collective-permute-start | bytes 393224 | tf_op jit(solution)/shard_map/ppermute | solution.py:18
  65.5 3.6 collective-permute-start.7
  69.1 3.4 collective-permute-done.6
  79.4 7.2 %collective-permute-done.8 = bf16[128,512]{0,1:T(8,128)(2,1)S(1)} collective-permute-done((bf16[128,512]{0,1:T(8,128)(2,1)S(1)}, bf16[128,512]{0,1:T(8,128)(2,1)S(1)}, u32[]{:S(2)}, u32[]{:S(2)}) %collective-permute-start.8) | collective-permute-done | bytes 131104 | tf_op jit(solution)/shard_map/ppermute | solution.py:18
  91.4 6.5 %collective-permute-done.10 = bf16[128,512]{0,1:T(8,128)(2,1)S(1)} collective-permute-done((bf16[128,512]{0,1:T(8,128)(2,1)S(1)}, bf16[128,512]{0,1:T(8,128)(2,1)S(1)}, u32[]{:S(2)}, u32[]{:S(2)}) %collective-permute-start.10) | collective-permute-done | bytes 131104 | tf_op jit(solution)/shard_map/ppermute | solution.py:18
  99.9 4.8 %collective-permute-start.16 = (bf16[128,2688]{1,0:T(8,128)(2,1)}, bf16[128,2688]{1,0:T(8,128)(2,1)}, u32[]{:S(2)}, u32[]{:S(2)}) collective-permute-start(bf16[128,2688]{1,0:T(8,128)(2,1)} %param.12), channel_id=1, source_target_pairs={{0,1},{1,0},{2,3},{3,2},{4,5},{5,4},{6,7},{7,6},{8,9},{9,8},{10,11... | collective-permute-start | bytes 2064392 | tf_op jit(solution)/shard_map/ppermute | solution.py:92
  104.8 4.5 %collective-permute-done.12 = bf16[128,512]{0,1:T(8,128)(2,1)S(1)} collective-permute-done((bf16[128,512]{0,1:T(8,128)(2,1)S(1)}, bf16[128,512]{0,1:T(8,128)(2,1)S(1)}, u32[]{:S(2)}, u32[]{:S(2)}) %collective-permute-start.12) | collective-permute-done | bytes 131104 | tf_op jit(solution)/shard_map/ppermute | solution.py:18
  113.0 11.9 %while.28 = (s32[]{:T(128)}, bf16[4,128,2,128]{1,3,2,0:T(8,128)(2,1)}, f32[4,2,128]{2,1,0:T(2,128)}, bf16[4,1152,128]{1,2,0:T(8,128)(2,1)S(1)}, bf16[4,1152,128]...) while((s32[]{:T(128)}, ...), condition=%wide.region_3.4_spmd.clone, body=%wide.region_0.3_spmd.clone.sunk | while | flops 153829120 | bytes 4571377 | solution.py:86
  124.9 8.1 %collective-permute-done.16 = bf16[128,2688]{1,0:T(8,128)(2,1)} collective-permute-done((bf16[128,2688]{1,0:T(8,128)(2,1)}, bf16[128,2688]{1,0:T(8,128)(2,1)}, u32[]{:S(2)}, u32[]{:S(2)}) %collective-permute-start.16) | collective-permute-done | bytes 688160 | tf_op jit(solution)/shard_map/ppermute | solution.py:92
  142.3 7.0 %all-to-all-start = ((bf16[8,128,1696]{1,2,0:T(8,128)(2,1)}), bf16[8,128,1696]{1,2,0:T(8,128)(2,1)}, u32[]{:S(2)}, u32[]{:S(2)}) async-start(bf16[8,128,1696]{1,2,0:T(8,128)(2,1)} %pad_maximum_fusion), calls=%async_computation | async-start | bytes 6946816 | tf_op jit(solution)/shard_map/all_to_all | solution.py:117
  149.6 41.8 %all-to-all-done = bf16[8,128,1696]{1,2,0:T(8,128)(2,1)} async-done(((bf16[8,128,1696]{1,2,0:T(8,128)(2,1)}), bf16[8,128,1696]{1,2,0:T(8,128)(2,1)}, u32[]{:S(2)}, u32[]{:S(2)}) %all-to-all-start) | async-done | bytes 3473440 | tf_op jit(solution)/shard_map/all_to_all | solution.py:117
  199.4 5.3 %multiply_bitcast_fusion = f32[8,1024,84]{1,2,0:T(8,128)} fusion(bf16[1024,8,84]{0,2,1:T(8,128)(2,1)} %reshape.108, bf16[1024,1024,1]{1,0,2:T(8,128)(2,1)} %bitcast.309), kind=kOutput, calls=%fused_computation.70 | convolution fusion | flops 1409974272 | bytes 6225920 | tf_op jit(solution)/shard_map/th,tak->ahk/dot_general | solution.py:122
  204.7 14.0 %reshape.111 = bf16[5376,1024]{1,0:T(8,128)(2,1)} reshape(bf16[64,84,1024]{2,1,0:T(8,128)(2,1)} %all-gather.3.cloned.1.call-done) | data formatting | bytes 22020096
  218.7 6.7 %fusion.64 = bf16[128,1024]{1,0:T(8,128)(2,1)S(1)} fusion(bf16[5376,1024]{1,0:T(8,128)(2,1)} %reshape.111, bf16[128,2688]{1,0:T(8,128)(2,1)} %collective-permute-done.16, bf16[128,2688]{1,0:T(8,128)(2,1)} %param.12, pred[]{:T(512)S(6)} %eq.3), kind=kOutput, calls=%fused_computation.81 | convolution fusion | flops 1415610368 | bytes 12648449 | tf_op jit(solution)/shard_map/dot_general | solution.py:98
  226.4 26.0 %while.29 = (s32[]{:T(128)}, bf16[4,128,2,128]{1,3,2,0:T(8,128)(2,1)}, f32[4,1152,128]{2,1,0:T(8,128)}, f32[4,1152,128]{2,1,0:T(8,128)}, bf16[4,1152,128]{2,1,0:...) while((s32[]{:T(128)}, ...), condition=%wide.region_6.7_spmd.clone, body=%wide.region_5.6_spmd.clone.sunk | while | flops 380469248 | bytes 8078613 | solution.py:130
  273.9 5.6 %collective-permute-done.27 = f32[128,512]{1,0:T(8,128)S(1)} collective-permute-done((f32[128,512]{1,0:T(8,128)S(1)}, f32[128,512]{1,0:T(8,128)S(1)}, u32[]{:S(2)}, u32[]{:S(2)}) %collective-permute-start.27) | collective-permute-done | bytes 262176 | tf_op jit(solution)/shard_map/ppermute | solution.py:18
  287.7 5.7 %collective-permute-done.29 = f32[128,512]{1,0:T(8,128)S(1)} collective-permute-done((f32[128,512]{1,0:T(8,128)S(1)}, f32[128,512]{1,0:T(8,128)S(1)}, u32[]{:S(2)}, u32[]{:S(2)}) %collective-permute-start.29) | collective-permute-done | bytes 262176 | tf_op jit(solution)/shard_map/ppermute | solution.py:18
  299.0 3.8 collective-permute-start.19
  304.8 4.5 %collective-permute-start.20 = (f32[128,512]{1,0:T(8,128)S(1)}, f32[128,512]{1,0:T(8,128)S(1)}, u32[]{:S(2)}, u32[]{:S(2)}) collective-permute-start(f32[128,512]{1,0:T(8,128)S(1)} %bitcast.322), channel_id=1, source_target_pairs={{8,0},{10,2},{12,4},{14,6},{16,8},{18,10},{20,12},{22,14},{24,16},... | collective-permute-start | bytes 786440 | tf_op jit(solution)/shard_map/ppermute | solution.py:18
  309.3 14.0 %collective-permute-done.32 = f32[128,512]{1,0:T(8,128)} collective-permute-done((f32[128,512]{1,0:T(8,128)}, f32[128,512]{1,0:T(8,128)}, u32[]{:S(2)}, u32[]{:S(2)}) %collective-permute-start.32) | collective-permute-done | bytes 262176 | tf_op jit(solution)/shard_map/ppermute | solution.py:18
  331.6 11.0 %collective-permute-start.24 = (f32[128,512]{1,0:T(8,128)S(1)}, f32[128,512]{1,0:T(8,128)S(1)}, u32[]{:S(2)}, u32[]{:S(2)}) collective-permute-start(f32[128,512]{1,0:T(8,128)S(1)} %bitcast.314), channel_id=1, source_target_pairs={{16,0},{18,2},{20,4},{22,6},{24,8},{26,10},{28,12},{30,14},{32,16}... | collective-permute-start | bytes 786440 | tf_op jit(solution)/shard_map/ppermute | solution.py:18
  346.3 5.6 %collective-permute-done.22 = f32[128,512]{1,0:T(8,128)S(1)} collective-permute-done((f32[128,512]{1,0:T(8,128)S(1)}, f32[128,512]{1,0:T(8,128)S(1)}, u32[]{:S(2)}, u32[]{:S(2)}) %collective-permute-start.22) | collective-permute-done | bytes 262176 | tf_op jit(solution)/shard_map/ppermute | solution.py:18
  351.9 5.1 %collective-permute-done.23 = f32[128,512]{1,0:T(8,128)S(1)} collective-permute-done((f32[128,512]{1,0:T(8,128)S(1)}, f32[128,512]{1,0:T(8,128)S(1)}, u32[]{:S(2)}, u32[]{:S(2)}) %collective-permute-start.23) | collective-permute-done | bytes 262176 | tf_op jit(solution)/shard_map/ppermute | solution.py:18
  357.0 15.1 %collective-permute-done.24 = f32[128,512]{1,0:T(8,128)S(1)} collective-permute-done((f32[128,512]{1,0:T(8,128)S(1)}, f32[128,512]{1,0:T(8,128)S(1)}, u32[]{:S(2)}, u32[]{:S(2)}) %collective-permute-start.24) | collective-permute-done | bytes 262176 | tf_op jit(solution)/shard_map/ppermute | solution.py:18
  (179 shorter events, 137.6 us)
Async XLA Ops:
  8.0 196.7 %all-gather.3.cloned.1.call-start = ((), (), s32[]{:S(2)}) async-start(), calls=%async_computation.3 | async-start | bytes 11714560 | tf_op jit(solution)/shard_map/all_gather | solution.py:100
  9.8 102.3 %collective-permute-start.15 = (bf16[128,512]{0,1:T(8,128)(2,1)S(1)}, bf16[128,512]{0,1:T(8,128)(2,1)}, u32[]{:S(2)}, u32[]{:S(2)}) collective-permute-start(bf16[128,512]{0,1:T(8,128)(2,1)S(1)} %copy.102), channel_id=1, source_target_pairs={{0,2},{2,4},{4,6},{6,8},{8,10},{10,12},{12,14},{14,16},{16,18},{18... | collective-permute-start | bytes 393224 | tf_op jit(solution)/shard_map/ppermute | solution.py:18
  11.7 99.4 %collective-permute-start.14 = (bf16[128,512]{0,1:T(8,128)(2,1)S(1)}, bf16[128,512]{0,1:T(8,128)(2,1)}, u32[]{:S(2)}, u32[]{:S(2)}) collective-permute-start(bf16[128,512]{0,1:T(8,128)(2,1)S(1)} %copy.102), channel_id=1, source_target_pairs={{0,4},{2,6},{4,8},{6,10},{8,12},{10,14},{12,16},{14,18},{16,20},{1... | collective-permute-start | bytes 393224 | tf_op jit(solution)/shard_map/ppermute | solution.py:18
  15.5 93.8 %collective-permute-start.13 = (bf16[128,512]{0,1:T(8,128)(2,1)S(1)}, bf16[128,512]{0,1:T(8,128)(2,1)S(1)}, u32[]{:S(2)}, u32[]{:S(2)}) collective-permute-start(bf16[128,512]{0,1:T(8,128)(2,1)S(1)} %copy.102), channel_id=1, source_target_pairs={{0,6},{2,8},{4,10},{6,12},{8,14},{10,16},{12,18},{14,20},{16,22},{... | collective-permute-start | bytes 393224 | tf_op jit(solution)/shard_map/ppermute | solution.py:18
  21.4 21.3 %collective-permute-start.1 = (bf16[128,512]{0,1:T(8,128)(2,1)S(1)}, bf16[128,512]{0,1:T(8,128)(2,1)S(1)}, u32[]{:S(2)}, u32[]{:S(2)}) collective-permute-start(bf16[128,512]{0,1:T(8,128)(2,1)S(1)} %copy.92), channel_id=1, source_target_pairs={{0,14},{2,16},{4,18},{6,20},{8,22},{10,24},{12,26},{14,28},{16,30}... | collective-permute-start | bytes 393224 | tf_op jit(solution)/shard_map/ppermute | solution.py:18
  25.7 11.2 %collective-permute-start = (bf16[128,512]{0,1:T(8,128)(2,1)S(1)}, bf16[128,512]{0,1:T(8,128)(2,1)S(1)}, u32[]{:S(2)}, u32[]{:S(2)}) collective-permute-start(bf16[128,512]{0,1:T(8,128)(2,1)S(1)} %copy.92), channel_id=1, source_target_pairs={{0,16},{2,18},{4,20},{6,22},{8,24},{10,26},{12,28},{14,30},{16,32}... | collective-permute-start | bytes 393224 | tf_op jit(solution)/shard_map/ppermute | solution.py:18
  36.9 11.5 %collective-permute-start.2 = (bf16[128,512]{0,1:T(8,128)(2,1)S(1)}, bf16[128,512]{0,1:T(8,128)(2,1)S(1)}, u32[]{:S(2)}, u32[]{:S(2)}) collective-permute-start(bf16[128,512]{0,1:T(8,128)(2,1)S(1)} %copy.92), channel_id=1, source_target_pairs={{0,12},{2,14},{4,16},{6,18},{8,20},{10,22},{12,24},{14,26},{16,28}... | collective-permute-start | bytes 393224 | tf_op jit(solution)/shard_map/ppermute | solution.py:18
  42.8 11.1 %collective-permute-start.3 = (bf16[128,512]{0,1:T(8,128)(2,1)S(1)}, bf16[128,512]{0,1:T(8,128)(2,1)S(1)}, u32[]{:S(2)}, u32[]{:S(2)}) collective-permute-start(bf16[128,512]{0,1:T(8,128)(2,1)S(1)} %copy.92), channel_id=1, source_target_pairs={{0,10},{2,12},{4,14},{6,16},{8,18},{10,20},{12,22},{14,24},{16,26}... | collective-permute-start | bytes 393224 | tf_op jit(solution)/shard_map/ppermute | solution.py:18
  53.9 11.6 %collective-permute-start.5 = (bf16[128,512]{0,1:T(8,128)(2,1)S(1)}, bf16[128,512]{0,1:T(8,128)(2,1)S(1)}, u32[]{:S(2)}, u32[]{:S(2)}) collective-permute-start(bf16[128,512]{0,1:T(8,128)(2,1)S(1)} %copy.92), channel_id=1, source_target_pairs={{0,6},{2,8},{4,10},{6,12},{8,14},{10,16},{12,18},{14,20},{16,22},{... | collective-permute-start | bytes 393224 | tf_op jit(solution)/shard_map/ppermute | solution.py:18
  59.3 13.1 %collective-permute-start.6 = (bf16[128,512]{0,1:T(8,128)(2,1)S(1)}, bf16[128,512]{0,1:T(8,128)(2,1)S(1)}, u32[]{:S(2)}, u32[]{:S(2)}) collective-permute-start(bf16[128,512]{0,1:T(8,128)(2,1)S(1)} %copy.92), channel_id=1, source_target_pairs={{0,4},{2,6},{4,8},{6,10},{8,12},{10,14},{12,16},{14,18},{16,20},{1... | collective-permute-start | bytes 393224 | tf_op jit(solution)/shard_map/ppermute | solution.py:18
  72.4 17.0 %collective-permute-start.9 = (bf16[128,512]{0,1:T(8,128)(2,1)S(1)}, bf16[128,512]{0,1:T(8,128)(2,1)S(1)}, u32[]{:S(2)}, u32[]{:S(2)}) collective-permute-start(bf16[128,512]{0,1:T(8,128)(2,1)S(1)} %copy.102), channel_id=1, source_target_pairs={{0,14},{2,16},{4,18},{6,20},{8,22},{10,24},{12,26},{14,28},{16,30}... | collective-permute-start | bytes 393224 | tf_op jit(solution)/shard_map/ppermute | solution.py:18
  86.6 11.3 %collective-permute-start.10 = (bf16[128,512]{0,1:T(8,128)(2,1)S(1)}, bf16[128,512]{0,1:T(8,128)(2,1)S(1)}, u32[]{:S(2)}, u32[]{:S(2)}) collective-permute-start(bf16[128,512]{0,1:T(8,128)(2,1)S(1)} %copy.102), channel_id=1, source_target_pairs={{0,12},{2,14},{4,16},{6,18},{8,20},{10,22},{12,24},{14,26},{16,28}... | collective-permute-start | bytes 393224 | tf_op jit(solution)/shard_map/ppermute | solution.py:18
  97.9 11.4 %collective-permute-start.12 = (bf16[128,512]{0,1:T(8,128)(2,1)S(1)}, bf16[128,512]{0,1:T(8,128)(2,1)S(1)}, u32[]{:S(2)}, u32[]{:S(2)}) collective-permute-start(bf16[128,512]{0,1:T(8,128)(2,1)S(1)} %copy.102), channel_id=1, source_target_pairs={{0,8},{2,10},{4,12},{6,14},{8,16},{10,18},{12,20},{14,22},{16,24},... | collective-permute-start | bytes 393224 | tf_op jit(solution)/shard_map/ppermute | solution.py:18
  99.9 33.2 %collective-permute-start.16 = (bf16[128,2688]{1,0:T(8,128)(2,1)}, bf16[128,2688]{1,0:T(8,128)(2,1)}, u32[]{:S(2)}, u32[]{:S(2)}) collective-permute-start(bf16[128,2688]{1,0:T(8,128)(2,1)} %param.12), channel_id=1, source_target_pairs={{0,1},{1,0},{2,3},{3,2},{4,5},{5,4},{6,7},{7,6},{8,9},{9,8},{10,11... | collective-permute-start | bytes 2064392 | tf_op jit(solution)/shard_map/ppermute | solution.py:92
  142.3 49.0 %all-to-all-start = ((bf16[8,128,1696]{1,2,0:T(8,128)(2,1)}), bf16[8,128,1696]{1,2,0:T(8,128)(2,1)}, u32[]{:S(2)}, u32[]{:S(2)}) async-start(bf16[8,128,1696]{1,2,0:T(8,128)(2,1)} %pad_maximum_fusion), calls=%async_computation | async-start | bytes 6946816 | tf_op jit(solution)/shard_map/all_to_all | solution.py:117
  149.4 224.7 %reduce-scatter.2.cloned.1.call-start = ((), (), s32[]{:S(2)}) async-start(), calls=%async_computation.2 | async-start | bytes 3244032 | tf_op jit(solution)/shard_map/reduce_scatter | solution.py:125
  254.2 11.4 %collective-permute-start.25 = (f32[128,512]{1,0:T(8,128)S(1)}, f32[128,512]{1,0:T(8,128)S(1)}, u32[]{:S(2)}, u32[]{:S(2)}) collective-permute-start(f32[128,512]{1,0:T(8,128)S(1)} %bitcast.324), channel_id=1, source_target_pairs={{2,0},{4,2},{6,4},{8,6},{10,8},{12,10},{14,12},{16,14},{18,16},{20... | collective-permute-start | bytes 786440 | tf_op jit(solution)/shard_map/ppermute | solution.py:18
  257.7 14.2 %collective-permute-start.26 = (f32[128,512]{1,0:T(8,128)S(1)}, f32[128,512]{1,0:T(8,128)S(1)}, u32[]{:S(2)}, u32[]{:S(2)}) collective-permute-start(f32[128,512]{1,0:T(8,128)S(1)} %bitcast.323), channel_id=1, source_target_pairs={{4,0},{6,2},{8,4},{10,6},{12,8},{14,10},{16,12},{18,14},{20,16},{2... | collective-permute-start | bytes 786440 | tf_op jit(solution)/shard_map/ppermute | solution.py:18
  259.8 19.6 %collective-permute-start.27 = (f32[128,512]{1,0:T(8,128)S(1)}, f32[128,512]{1,0:T(8,128)S(1)}, u32[]{:S(2)}, u32[]{:S(2)}) collective-permute-start(f32[128,512]{1,0:T(8,128)S(1)} %bitcast.321), channel_id=1, source_target_pairs={{6,0},{8,2},{10,4},{12,6},{14,8},{16,10},{18,12},{20,14},{22,16},{... | collective-permute-start | bytes 786440 | tf_op jit(solution)/shard_map/ppermute | solution.py:18
  261.7 24.0 %collective-permute-start.28 = (f32[128,512]{1,0:T(8,128)S(1)}, f32[128,512]{1,0:T(8,128)S(1)}, u32[]{:S(2)}, u32[]{:S(2)}) collective-permute-start(f32[128,512]{1,0:T(8,128)S(1)} %bitcast.318), channel_id=1, source_target_pairs={{8,0},{10,2},{12,4},{14,6},{16,8},{18,10},{20,12},{22,14},{24,16},... | collective-permute-start | bytes 786440 | tf_op jit(solution)/shard_map/ppermute | solution.py:18
  263.7 29.7 %collective-permute-start.29 = (f32[128,512]{1,0:T(8,128)S(1)}, f32[128,512]{1,0:T(8,128)S(1)}, u32[]{:S(2)}, u32[]{:S(2)}) collective-permute-start(f32[128,512]{1,0:T(8,128)S(1)} %bitcast.315), channel_id=1, source_target_pairs={{10,0},{12,2},{14,4},{16,6},{18,8},{20,10},{22,12},{24,14},{26,16}... | collective-permute-start | bytes 786440 | tf_op jit(solution)/shard_map/ppermute | solution.py:18
  265.6 33.4 %collective-permute-start.30 = (f32[128,512]{1,0:T(8,128)S(1)}, f32[128,512]{1,0:T(8,128)S(1)}, u32[]{:S(2)}, u32[]{:S(2)}) collective-permute-start(f32[128,512]{1,0:T(8,128)S(1)} %bitcast.313), channel_id=1, source_target_pairs={{12,0},{14,2},{16,4},{18,6},{20,8},{22,10},{24,12},{26,14},{28,16}... | collective-permute-start | bytes 786440 | tf_op jit(solution)/shard_map/ppermute | solution.py:18
  271.9 32.8 %collective-permute-start.31 = (f32[128,512]{1,0:T(8,128)}, f32[128,512]{1,0:T(8,128)}, u32[]{:S(2)}, u32[]{:S(2)}) collective-permute-start(f32[128,512]{1,0:T(8,128)} %bitcast.244), channel_id=1, source_target_pairs={{14,0},{16,2},{18,4},{20,6},{22,8},{24,10},{26,12},{28,14},{30,16}... | collective-permute-start | bytes 786440 | tf_op jit(solution)/shard_map/ppermute | solution.py:18
  279.4 43.9 %collective-permute-start.32 = (f32[128,512]{1,0:T(8,128)}, f32[128,512]{1,0:T(8,128)}, u32[]{:S(2)}, u32[]{:S(2)}) collective-permute-start(f32[128,512]{1,0:T(8,128)} %bitcast.243), channel_id=1, source_target_pairs={{16,0},{18,2},{20,4},{22,6},{24,8},{26,10},{28,12},{30,14},{32,16}... | collective-permute-start | bytes 786440 | tf_op jit(solution)/shard_map/ppermute | solution.py:18
  285.8 39.5 %collective-permute-start.17 = (f32[128,512]{1,0:T(8,128)}, f32[128,512]{1,0:T(8,128)}, u32[]{:S(2)}, u32[]{:S(2)}) collective-permute-start(f32[128,512]{1,0:T(8,128)} %bitcast.258), channel_id=1, source_target_pairs={{2,0},{4,2},{6,4},{8,6},{10,8},{12,10},{14,12},{16,14},{18,16},{20... | collective-permute-start | bytes 786440 | tf_op jit(solution)/shard_map/ppermute | solution.py:18
  293.3 33.8 %collective-permute-start.18 = (f32[128,512]{1,0:T(8,128)}, f32[128,512]{1,0:T(8,128)}, u32[]{:S(2)}, u32[]{:S(2)}) collective-permute-start(f32[128,512]{1,0:T(8,128)} %bitcast.257), channel_id=1, source_target_pairs={{4,0},{6,2},{8,4},{10,6},{12,8},{14,10},{16,12},{18,14},{20,16},{2... | collective-permute-start | bytes 786440 | tf_op jit(solution)/shard_map/ppermute | solution.py:18
  299.0 32.6 %collective-permute-start.19 = (f32[128,512]{1,0:T(8,128)}, f32[128,512]{1,0:T(8,128)}, u32[]{:S(2)}, u32[]{:S(2)}) collective-permute-start(f32[128,512]{1,0:T(8,128)} %bitcast.256), channel_id=1, source_target_pairs={{6,0},{8,2},{10,4},{12,6},{14,8},{16,10},{18,12},{20,14},{22,16},{... | collective-permute-start | bytes 786440 | tf_op jit(solution)/shard_map/ppermute | solution.py:18
  304.8 39.7 %collective-permute-start.20 = (f32[128,512]{1,0:T(8,128)S(1)}, f32[128,512]{1,0:T(8,128)S(1)}, u32[]{:S(2)}, u32[]{:S(2)}) collective-permute-start(f32[128,512]{1,0:T(8,128)S(1)} %bitcast.322), channel_id=1, source_target_pairs={{8,0},{10,2},{12,4},{14,6},{16,8},{18,10},{20,12},{22,14},{24,16},... | collective-permute-start | bytes 786440 | tf_op jit(solution)/shard_map/ppermute | solution.py:18
  323.3 23.0 %collective-permute-start.21 = (f32[128,512]{1,0:T(8,128)S(1)}, f32[128,512]{1,0:T(8,128)S(1)}, u32[]{:S(2)}, u32[]{:S(2)}) collective-permute-start(f32[128,512]{1,0:T(8,128)S(1)} %bitcast.319), channel_id=1, source_target_pairs={{10,0},{12,2},{14,4},{16,6},{18,8},{20,10},{22,12},{24,14},{26,16}... | collective-permute-start | bytes 786440 | tf_op jit(solution)/shard_map/ppermute | solution.py:18
  325.2 26.7 %collective-permute-start.22 = (f32[128,512]{1,0:T(8,128)S(1)}, f32[128,512]{1,0:T(8,128)S(1)}, u32[]{:S(2)}, u32[]{:S(2)}) collective-permute-start(f32[128,512]{1,0:T(8,128)S(1)} %bitcast.317), channel_id=1, source_target_pairs={{12,0},{14,2},{16,4},{18,6},{20,8},{22,10},{24,12},{26,14},{28,16}... | collective-permute-start | bytes 786440 | tf_op jit(solution)/shard_map/ppermute | solution.py:18
  327.2 29.9 %collective-permute-start.23 = (f32[128,512]{1,0:T(8,128)S(1)}, f32[128,512]{1,0:T(8,128)S(1)}, u32[]{:S(2)}, u32[]{:S(2)}) collective-permute-start(f32[128,512]{1,0:T(8,128)S(1)} %bitcast.316), channel_id=1, source_target_pairs={{14,0},{16,2},{18,4},{20,6},{22,8},{24,10},{26,12},{28,14},{30,16}... | collective-permute-start | bytes 786440 | tf_op jit(solution)/shard_map/ppermute | solution.py:18
  331.6 40.5 %collective-permute-start.24 = (f32[128,512]{1,0:T(8,128)S(1)}, f32[128,512]{1,0:T(8,128)S(1)}, u32[]{:S(2)}, u32[]{:S(2)}) collective-permute-start(f32[128,512]{1,0:T(8,128)S(1)} %bitcast.314), channel_id=1, source_target_pairs={{16,0},{18,2},{20,4},{22,6},{24,8},{26,10},{28,12},{30,14},{32,16}... | collective-permute-start | bytes 786440 | tf_op jit(solution)/shard_map/ppermute | solution.py:18
  (9 other events, 96.9 us)
Sparse Core Ops, SparseCore 0:
  10.5 129.8 all-gather.2
Sparse Core Ops, SparseCore 1:
  204.8 70.9 reduce-scatter.1
